TPU v7x, 512 devices: a whole 4x4x16 slice. The times are simulated.
512 devices in a mesh: dp: 8 (over x, y_hi), expert: 64 (over y_lo, z, core).
Axes of the slice: x: 4, y: 4 (y_hi: 2, y_lo: 2; y = y_hi * 2 + y_lo), z: 16, core: 2. Of those that a mesh axis runs over, the one named last changes fastest.
Arguments:
- tokens: bfloat16 [65536, 2048], P(('dp', 'expert')), may hold values from -6 to 6
- out_grad: bfloat16 [65536, 2048], P(('dp', 'expert')), may hold values from -6 to 6
- combine: float32 [65536, 2], P(('dp', 'expert')), may hold values from 0.1 to 1
- expert_ids: int32 [65536, 2], P(('dp', 'expert')), may hold values from 0 to 63, all different within a row; in each aligned block of 128 rows (0 to 127, 128 to 255, ...) at most 5 rows name the same one
- gate_weight: bfloat16 [64, 2048, 768], P('expert', 'dp'), may hold values from -0.125 to 0.125
- up_weight: bfloat16 [64, 2048, 768], P('expert', 'dp'), may hold values from -0.125 to 0.125
- down_weight: bfloat16 [64, 2048, 768], P('expert', 'dp'), may hold values from -0.21875 to 0.21875
Outputs:
- token_grad: bfloat16 [65536, 2048], P(('dp', 'expert'))
- down_grad: bfloat16 [64, 2048, 768], P('expert', 'dp')
Inputs may be any that keep to these rules, and one draw needn't show every extreme that they name: `expert_ids`: each row names 2 different experts. Among the 128 rows of one device no expert is named more than 5 times, a bound that some block reaches.
All inputs are finite; a program needn't handle non-finite values.
Results may differ from a plain program's by a relative error of at most 0.012.
Values may be sent and summed in bfloat16 or wider, within the bound.
No kernel may reach another device: no remote copies, remote signals or barrier semaphores. Data moves between devices by JAX's collectives and lax.ppermute only.
A program may use at most 64 MiB of HBM per device.

v0:
```python
import jax
import jax.numpy as jnp
from jax import lax
from jax.sharding import Mesh
from jax.sharding import PartitionSpec as P

TOP = 2
CAP = 5
SUB = ("ylo", "z", "core")
ROWS = ("dp",) + SUB
SWAP = [(0, 1), (1, 0)]


def swap_half(x, axis_name, dim):
    stay = lax.index_in_dim(x, 0, dim, keepdims=True)
    go = lax.index_in_dim(x, 1, dim, keepdims=True)
    got = lax.ppermute(go, axis_name, SWAP)
    return jnp.concatenate([stay, got], dim)


def forward_move(x, z_first):
    if z_first:
        x = lax.all_to_all(x, "z", 2, 2, tiled=True)
    x = swap_half(x, "core", 0)
    x = swap_half(x, "ylo", 1)
    if not z_first:
        x = lax.all_to_all(x, "z", 2, 2, tiled=True)
    return x


def backward_move(x, z_first):
    if z_first:
        x = lax.all_to_all(x, "z", 2, 2, tiled=True)
    x = swap_half(x, "ylo", 1)
    x = swap_half(x, "core", 0)
    if not z_first:
        x = lax.all_to_all(x, "z", 2, 2, tiled=True)
    return x


def body(tokens, out_grad, combine, expert_ids, gate_weight, up_weight, down_weight):
    token_rows = tokens.shape[0]
    width = tokens.shape[1]
    n_ylo, n_z, n_core = (lax.axis_size(a) for a in SUB)
    expert_count = n_ylo * n_z * n_core
    capacity = CAP
    positions = expert_count * capacity
    w_gate = lax.all_gather(gate_weight, "dp", axis=1, tiled=True)[0]
    w_up = lax.all_gather(up_weight, "dp", axis=1, tiled=True)[0]
    w_down = lax.all_gather(down_weight, "dp", axis=1, tiled=True)[0]
    flat_ids = expert_ids.reshape(-1)
    onehot = (flat_ids[:, None] == jnp.arange(expert_count, dtype=jnp.int32)[None, :]).astype(jnp.int32)
    earlier = jnp.cumsum(onehot, axis=0) - onehot
    slot_index = jnp.sum(earlier * onehot, axis=1)
    my_core = lax.axis_index("core")
    my_ylo = lax.axis_index("ylo")
    e_core = flat_ids % n_core
    e_z = (flat_ids // n_core) % n_z
    e_ylo = flat_ids // (n_core * n_z)
    rel = ((e_core ^ my_core) * n_ylo + (e_ylo ^ my_ylo)) * n_z + e_z
    target = rel * capacity + slot_index
    matches = target[None, :] == jnp.arange(positions, dtype=jnp.int32)[:, None]
    picker = jnp.sum(
        matches.reshape(positions, token_rows, TOP).astype(jnp.float32), axis=2
    ).astype(jnp.bfloat16)
    slot_weight = jnp.sum(jnp.where(matches, combine.reshape(-1)[None, :], jnp.float32(0.0)), axis=1)
    row_send = jnp.dot(picker, tokens, preferred_element_type=jnp.float32).astype(jnp.bfloat16)
    picked_grad = jnp.dot(picker, out_grad, preferred_element_type=jnp.float32)
    grad_send = (slot_weight[:, None] * picked_grad).astype(jnp.bfloat16)
    block = (n_core, n_ylo, n_z, capacity, width)
    rows_in = forward_move(row_send.reshape(block), True).reshape(positions, width)
    grads_in = forward_move(grad_send.reshape(block), False).reshape(positions, width)
    gate_pre = jnp.dot(rows_in, w_gate, preferred_element_type=jnp.float32)
    up_pre = jnp.dot(rows_in, w_up, preferred_element_type=jnp.float32)
    sigmoid_gate = jax.nn.sigmoid(gate_pre)
    silu_gate = gate_pre * sigmoid_gate
    hidden = (silu_gate * up_pre).astype(jnp.bfloat16)
    hidden_grad = jnp.dot(grads_in, w_down, preferred_element_type=jnp.float32)
    gate_grad = (
        hidden_grad * up_pre * sigmoid_gate * (1.0 + gate_pre * (1.0 - sigmoid_gate))
    ).astype(jnp.bfloat16)
    up_grad = (hidden_grad * silu_gate).astype(jnp.bfloat16)
    contract_hidden = (((1,), (1,)), ((), ()))
    half = width // 2
    pieces = []
    for h in range(2):
        cols = slice(h * half, (h + 1) * half)
        row_grad = (
            lax.dot_general(gate_grad, w_gate[cols], contract_hidden, preferred_element_type=jnp.float32)
            + lax.dot_general(up_grad, w_up[cols], contract_hidden, preferred_element_type=jnp.float32)
        ).astype(jnp.bfloat16)
        back_rows = backward_move(row_grad.reshape(block[:-1] + (half,)), h == 0)
        pieces.append(
            lax.dot_general(
                picker,
                back_rows.reshape(positions, half),
                (((0,), (0,)), ((), ())),
                preferred_element_type=jnp.float32,
            ).astype(jnp.bfloat16)
        )
    token_grad = jnp.concatenate(pieces, 1)
    down_grad = lax.psum_scatter(
        lax.dot_general(
            grads_in, hidden, (((0,), (0,)), ((), ())), preferred_element_type=jnp.float32
        ).astype(jnp.bfloat16),
        "dp",
        scatter_dimension=0,
        tiled=True,
    )
    return (token_grad, down_grad[None])


def solution(mesh):
    n_dp, n_expert = mesh.devices.shape
    fine = Mesh(mesh.devices.reshape(n_dp, 2, n_expert // 4, 2), ("dp",) + SUB)
    rows = P(ROWS, None)
    weights = P(SUB, "dp", None)
    return jax.shard_map(
        body,
        mesh=fine,
        in_specs=(rows, rows, rows, rows, weights, weights, weights),
        out_specs=(rows, weights),
        check_vma=False,
    )
```

profile of v0, /device:TPU:6, one launch (start us, length us, event | category | flops | bytes accessed | tf_op | source)
XLA Modules:
  0.0 368.4 jit_solution(2858268402783092112)
XLA Ops:
  7.2 0.7 all-gather.4.cloned.1.call-update
  8.0 0.7 all-gather.6.cloned.1.call-update
  8.7 0.8 copy.84
  9.7 0.7 broadcast_compare_fusion
  10.4 0.6 reduce-window.6
  12.4 0.6 reshape.143
  13.0 2.6 copy.103
  15.6 15.3 %all-to-all-start.1 = ((bf16[2,2,16,5,2048]{4,1,3,0,2:T(2,128)(2,1)}), bf16[2,2,16,5,2048]{4,1,3,0,2:T(2,128)(2,1)S(1)}, u32[]{:S(2)}, u32[]{:S(2)}) async-start(bf16[2,2,16,5,2048]{4,1,3,0,2:T(2,128)(2,1)} %copy.103), calls=%async_computation.1 | async-start | bytes 2621440 | tf_op jit(solution)/shard_map/all_to_all | solution.py:23
  31.4 0.5 fusion.6
  31.9 1.0 fusion.43
  32.9 1.4 slice.89
  34.3 1.3 copy.97
  35.6 1.9 collective-permute-start
  37.9 2.1 collective-permute-done
  39.9 1.5 copy_dynamic-update-slice_fusion
  42.1 3.5 collective-permute-start.1
  45.6 15.2 %collective-permute-done.1 = bf16[2,1,16,5,2048]{4,2,3,1,0:T(8,128)(2,1)S(1)} collective-permute-done((bf16[2,1,16,5,2048]{4,2,3,1,0:T(8,128)(2,1)S(1)}, bf16[2,1,16,5,2048]{4,2,3,1,0:T(8,128)(2,1)S(1)}, u32[]{:S(2)}, u32[]{:S(2)}) %collective-permute-start.1) | collective-permute-done | bytes 655392 | tf_op jit(solution)/shard_map/ppermute | solution.py:17
  61.6 2.6 copy.101
  64.2 29.6 %all-to-all-done.1 = bf16[2,2,16,5,2048]{4,1,3,0,2:T(2,128)(2,1)S(1)} async-done(((bf16[2,2,16,5,2048]{4,1,3,0,2:T(2,128)(2,1)}), bf16[2,2,16,5,2048]{4,1,3,0,2:T(2,128)(2,1)S(1)}, u32[]{:S(2)}, u32[]{:S(2)}) %all-to-all-start.1) | async-done | bytes 1310752 | tf_op jit(solution)/shard_map/all_to_all | solution.py:23
  93.8 6.2 %all-to-all-start = ((bf16[2,2,16,5,2048]{4,1,3,0,2:T(2,128)(2,1)}), bf16[2,2,16,5,2048]{4,1,3,0,2:T(2,128)(2,1)S(1)}, u32[]{:S(2)}, u32[]{:S(2)}) async-start(bf16[2,2,16,5,2048]{4,1,3,0,2:T(2,128)(2,1)} %copy.101), calls=%async_computation | async-start | bytes 2621440 | tf_op jit(solution)/shard_map/all_to_all | solution.py:27
  100.1 0.7 all-gather.8.cloned.1.call-update
  100.8 0.9 fusion.42
  102.0 2.1 collective-permute-start.2
  104.1 1.9 collective-permute-done.2
  106.0 0.7 copy.105
  106.6 3.2 slice_maximum_fusion
  109.8 1.6 copy.106
  111.4 3.5 collective-permute-start.3
  114.8 46.2 %all-to-all-done = bf16[2,2,16,5,2048]{4,1,3,0,2:T(2,128)(2,1)S(1)} async-done(((bf16[2,2,16,5,2048]{4,1,3,0,2:T(2,128)(2,1)}), bf16[2,2,16,5,2048]{4,1,3,0,2:T(2,128)(2,1)S(1)}, u32[]{:S(2)}, u32[]{:S(2)}) %all-to-all-start) | async-done | bytes 1310752 | tf_op jit(solution)/shard_map/all_to_all | solution.py:27
  161.0 0.6 copy.102
  161.7 0.6 reshape.142
  162.3 2.9 copy.107
  165.2 3.0 pad_maximum_fusion.2
  168.2 0.6 copy.108
  168.9 1.4 reshape.144
  170.3 4.2 %fusion.4 = f32[320,768]{1,0:T(8,128)} fusion(bf16[320,2048]{1,0:T(8,128)(2,1)S(1)} %reshape.142, bf16[1,2048,768]{2,1,0:T(8,128)(2,1)} %all-gather.4.cloned.1.call-done), kind=kOutput, calls=%fused_computation.5 | convolution fusion | flops 1006632960 | bytes 5439488 | tf_op jit(solution)/shard_map/dot_general | solution.py:78
  174.5 1.9 all-gather.6.cloned.1.call-done
  176.4 4.0 %fusion.2 = f32[320,768]{1,0:T(8,128)} fusion(bf16[320,2048]{1,0:T(8,128)(2,1)S(1)} %copy-done.7, bf16[1,2048,768]{2,1,0:T(8,128)(2,1)} %all-gather.6.cloned.1.call-done), kind=kOutput, calls=%fused_computation.3 | convolution fusion | flops 1006632960 | bytes 5439488 | tf_op jit(solution)/shard_map/dot_general | solution.py:74
  180.4 76.2 %all-gather.8.cloned.1.call-done = bf16[1,2048,768]{2,1,0:T(8,128)(2,1)} async-done(((bf16[1,256,768]{2,1,0:T(8,128)(2,1)}), bf16[1,2048,768]{2,1,0:T(8,128)(2,1)}) %all-gather.8.cloned.1.call-update) | async-done | bytes 3145744 | tf_op jit(solution)/shard_map/all_gather | solution.py:48
  256.6 4.1 %multiply_convert_fusion.2 = (bf16[320,768]{1,0:T(8,128)(2,1)S(1)}, bf16[320,768]{1,0:T(8,128)(2,1)S(1)}, f32[320,768]{1,0:T(8,128)S(1)}) fusion(f32[320,768]{1,0:T(8,128)S(1)} %copy-done.10, f32[320,768]{1,0:T(8,128)} %fusion.2, bf16[320,2048]{1,0:T(8,128)(2,1)} %reshape.144, bf16[1,2048,768]{2,1,0:T(8,128)(2,1)} %all-gather.8.cloned.1.call-done), kind=kOutput, calls=%fused_computation.34 | convolution fusion | flops 1009827840 | bytes 8388608 | tf_op jit(solution)/shard_map/dot_general | solution.py:73
  260.7 3.6 convolution_convert_fusion
  264.4 2.3 fusion.9
  266.7 0.7 fusion.14
  267.7 1.6 copy.109
  269.3 12.3 %all-to-all-start.2 = ((bf16[2,2,16,5,1024]{4,1,3,0,2:T(2,128)(2,1)}), bf16[2,2,16,5,1024]{4,1,3,0,2:T(2,128)(2,1)S(1)}, u32[]{:S(2)}, u32[]{:S(2)}) async-start(bf16[2,2,16,5,1024]{4,1,3,0,2:T(2,128)(2,1)} %copy.109), calls=%async_computation.2 | async-start | bytes 1310720 | tf_op jit(solution)/shard_map/all_to_all | solution.py:33
  281.6 2.3 fusion.7
  283.9 0.7 fusion.13
  285.0 2.5 collective-permute-start.6
  287.5 15.7 %collective-permute-done.6 = bf16[2,1,16,5,1024]{4,3,2,1,0:T(8,128)(2,1)S(1)} collective-permute-done((bf16[2,1,16,5,1024]{4,3,2,1,0:T(8,128)(2,1)S(1)}, bf16[2,1,16,5,1024]{4,3,2,1,0:T(8,128)(2,1)S(1)}, u32[]{:S(2)}, u32[]{:S(2)}) %collective-permute-start.6) | collective-permute-done | bytes 327712 | tf_op jit(solution)/shard_map/ppermute | solution.py:17
  303.4 1.9 collective-permute-start.7
  305.4 1.9 collective-permute-done.7
  307.5 1.6 copy.113
  309.1 4.0 %all-to-all-done.2 = bf16[2,2,16,5,1024]{4,1,3,0,2:T(2,128)(2,1)S(1)} async-done(((bf16[2,2,16,5,1024]{4,1,3,0,2:T(2,128)(2,1)}), bf16[2,2,16,5,1024]{4,1,3,0,2:T(2,128)(2,1)S(1)}, u32[]{:S(2)}, u32[]{:S(2)}) %all-to-all-start.2) | async-done | bytes 655392 | tf_op jit(solution)/shard_map/all_to_all | solution.py:33
  313.1 8.0 %all-to-all-start.3 = ((bf16[2,2,16,5,1024]{4,1,3,0,2:T(2,128)(2,1)}), bf16[2,2,16,5,1024]{4,1,3,0,2:T(2,128)(2,1)S(1)}, u32[]{:S(2)}, u32[]{:S(2)}) async-start(bf16[2,2,16,5,1024]{4,1,3,0,2:T(2,128)(2,1)} %copy.113), calls=%async_computation.3 | async-start | bytes 1310720 | tf_op jit(solution)/shard_map/all_to_all | solution.py:37
  321.0 0.9 fusion.45
  322.1 2.8 collective-permute-start.4
  324.9 8.4 %collective-permute-done.4 = bf16[2,1,16,5,1024]{4,2,3,1,0:T(8,128)(2,1)S(1)} collective-permute-done((bf16[2,1,16,5,1024]{4,2,3,1,0:T(8,128)(2,1)S(1)}, bf16[2,1,16,5,1024]{4,2,3,1,0:T(8,128)(2,1)S(1)}, u32[]{:S(2)}, u32[]{:S(2)}) %collective-permute-start.4) | collective-permute-done | bytes 327712 | tf_op jit(solution)/shard_map/ppermute | solution.py:17
  333.3 0.5 copy.111
  333.8 1.4 fusion.17
  335.1 1.9 collective-permute-start.5
  337.1 17.7 %all-to-all-done.3 = bf16[2,2,16,5,1024]{4,1,3,0,2:T(2,128)(2,1)S(1)} async-done(((bf16[2,2,16,5,1024]{4,1,3,0,2:T(2,128)(2,1)}), bf16[2,2,16,5,1024]{4,1,3,0,2:T(2,128)(2,1)S(1)}, u32[]{:S(2)}, u32[]{:S(2)}) %all-to-all-start.3) | async-done | bytes 655392 | tf_op jit(solution)/shard_map/all_to_all | solution.py:37
  355.3 0.8 pad_maximum_fusion.4
  357.4 0.8 pad_maximum_fusion.6
  358.2 3.7 %reduce-scatter.2.cloned.1.call-done = bf16[256,768]{1,0:T(8,128)(2,1)} async-done(((bf16[2048,768]{1,0:T(8,128)(2,1)}), bf16[256,768]{1,0:T(8,128)(2,1)}) %reduce-scatter.2.cloned.1.call-update) | async-done | bytes 393232 | tf_op jit(solution)/shard_map/reduce_scatter | solution.py:102
  (68 shorter events, 7.4 us)
Async XLA Ops:
  7.2 4.8 %copy-start = (bf16[128,2048]{1,0:T(8,128)(2,1)S(1)}, bf16[128,2048]{1,0:T(8,128)(2,1)}, u32[]{:S(2)}) copy-start(bf16[128,2048]{1,0:T(8,128)(2,1)} %param.7) | copy-start | bytes 1572868
  7.2 163.1 %all-gather.4.cloned.1.call-start = ((), (), s32[]{:S(2)}) async-start(), calls=%async_computation.5 | async-start | bytes 3538944 | tf_op jit(solution)/shard_map/all_gather | solution.py:50
  7.9 168.4 %all-gather.6.cloned.1.call-start = ((), (), s32[]{:S(2)}) async-start(), calls=%async_computation.6 | async-start | bytes 3538944 | tf_op jit(solution)/shard_map/all_gather | solution.py:49
  15.6 15.3 %copy-start.9 = (f32[128,2]{0,1:T(2,128)S(1)}, f32[128,2]{0,1:T(2,128)}, u32[]{:S(2)}) copy-start(f32[128,2]{0,1:T(2,128)} %param.9) | copy-start | bytes 3076
  15.6 15.8 %copy-start.8 = (bf16[128,2048]{1,0:T(8,128)(2,1)S(1)}, bf16[128,2048]{1,0:T(8,128)(2,1)}, u32[]{:S(2)}) copy-start(bf16[128,2048]{1,0:T(8,128)(2,1)} %param.8) | copy-start | bytes 1572868
  15.6 78.2 %all-to-all-start.1 = ((bf16[2,2,16,5,2048]{4,1,3,0,2:T(2,128)(2,1)}), bf16[2,2,16,5,2048]{4,1,3,0,2:T(2,128)(2,1)S(1)}, u32[]{:S(2)}, u32[]{:S(2)}) async-start(bf16[2,2,16,5,2048]{4,1,3,0,2:T(2,128)(2,1)} %copy.103), calls=%async_computation.1 | async-start | bytes 2621440 | tf_op jit(solution)/shard_map/all_to_all | solution.py:23
  35.6 4.3 %collective-permute-start = (bf16[1,2,16,5,2048]{4,2,3,1,0:T(8,128)(2,1)}, bf16[1,2,16,5,2048]{4,2,3,1,0:T(8,128)(2,1)}, u32[]{:S(2)}, u32[]{:S(2)}) collective-permute-start(bf16[1,2,16,5,2048]{4,2,3,1,0:T(8,128)(2,1)} %copy.97), channel_id=1, source_target_pairs={{0,1},{1,0},{2,3},{3,2},{4,5},{5,4},{6,7},{7,6},{8,9},{9,8},{10,11... | collective-permute-start | bytes 1966088 | tf_op jit(solution)/shard_map/ppermute | solution.py:17
  42.1 18.7 %collective-permute-start.1 = (bf16[2,1,16,5,2048]{4,2,3,1,0:T(8,128)(2,1)S(1)}, bf16[2,1,16,5,2048]{4,2,3,1,0:T(8,128)(2,1)S(1)}, u32[]{:S(2)}, u32[]{:S(2)}) collective-permute-start(bf16[2,1,16,5,2048]{4,2,3,1,0:T(8,128)(2,1)S(1)} %copy.99), channel_id=1, source_target_pairs={{0,32},{32,0},{1,33},{33,1},{2,34},{34,2},{3,35},{35,3},{4,36},{36... | collective-permute-start | bytes 1966088 | tf_op jit(solution)/shard_map/ppermute | solution.py:17
  93.8 67.2 %all-to-all-start = ((bf16[2,2,16,5,2048]{4,1,3,0,2:T(2,128)(2,1)}), bf16[2,2,16,5,2048]{4,1,3,0,2:T(2,128)(2,1)S(1)}, u32[]{:S(2)}, u32[]{:S(2)}) async-start(bf16[2,2,16,5,2048]{4,1,3,0,2:T(2,128)(2,1)} %copy.101), calls=%async_computation | async-start | bytes 2621440 | tf_op jit(solution)/shard_map/all_to_all | solution.py:27
  100.1 156.6 %all-gather.8.cloned.1.call-start = ((), (), s32[]{:S(2)}) async-start(), calls=%async_computation.7 | async-start | bytes 3538944 | tf_op jit(solution)/shard_map/all_gather | solution.py:48
  100.8 261.1 %reduce-scatter.2.cloned.1.call-start = ((), (), s32[]{:S(2)}) async-start(), calls=%async_computation.8 | async-start | bytes 3538944 | tf_op jit(solution)/shard_map/reduce_scatter | solution.py:102
  102.0 4.0 %collective-permute-start.2 = (bf16[1,2,16,5,2048]{4,2,3,1,0:T(8,128)(2,1)S(1)}, bf16[1,2,16,5,2048]{4,2,3,1,0:T(8,128)(2,1)S(1)}, u32[]{:S(2)}, u32[]{:S(2)}) collective-permute-start(bf16[1,2,16,5,2048]{4,2,3,1,0:T(8,128)(2,1)S(1)} %copy.104), channel_id=1, source_target_pairs={{0,1},{1,0},{2,3},{3,2},{4,5},{5,4},{6,7},{7,6},{8,9},{9,8},{10,11... | collective-permute-start | bytes 1966088 | tf_op jit(solution)/shard_map/ppermute | solution.py:17
  111.4 50.9 %collective-permute-start.3 = (bf16[2,1,16,5,2048]{4,2,3,1,0:T(8,128)(2,1)}, bf16[2,1,16,5,2048]{4,2,3,1,0:T(8,128)(2,1)}, u32[]{:S(2)}, u32[]{:S(2)}) collective-permute-start(bf16[2,1,16,5,2048]{4,2,3,1,0:T(8,128)(2,1)} %copy.106), channel_id=1, source_target_pairs={{0,32},{32,0},{1,33},{33,1},{2,34},{34,2},{3,35},{35,3},{4,36},{36... | collective-permute-start | bytes 1966088 | tf_op jit(solution)/shard_map/ppermute | solution.py:17
  162.3 8.0 %copy-start.5 = (bf16[320,2048]{1,0:T(8,128)(2,1)}, bf16[320,2048]{1,0:T(8,128)(2,1)S(1)}, u32[]{:S(2)}) copy-start(bf16[320,2048]{1,0:T(8,128)(2,1)S(1)} %reshape.142) | copy-start | bytes 3932164
  162.3 3.0 copy-start.2
  170.3 6.1 %copy-start.7 = (bf16[320,2048]{1,0:T(8,128)(2,1)S(1)}, bf16[320,2048]{1,0:T(8,128)(2,1)}, u32[]{:S(2)}) copy-start(bf16[320,2048]{1,0:T(8,128)(2,1)} %reshape.144) | copy-start | bytes 3932164
  174.5 82.1 %copy-start.10 = (f32[320,768]{1,0:T(8,128)S(1)}, f32[320,768]{1,0:T(8,128)}, u32[]{:S(2)}) copy-start(f32[320,768]{1,0:T(8,128)} %fusion.4) | copy-start | bytes 2949124
  180.4 80.3 %copy-start.6 = (bf16[320,2048]{1,0:T(8,128)(2,1)S(1)}, bf16[320,2048]{1,0:T(8,128)(2,1)}, u32[]{:S(2)}) copy-start(bf16[320,2048]{1,0:T(8,128)(2,1)} %copy-done.5) | copy-start | bytes 3932164
  256.6 4.1 %copy-start.11 = (f32[320,768]{1,0:T(8,128)S(1)}, f32[320,768]{1,0:T(8,128)}, u32[]{:S(2)}) copy-start(f32[320,768]{1,0:T(8,128)} %fusion.2) | copy-start | bytes 2949124
  264.4 2.4 copy-start.3
  269.3 43.8 %all-to-all-start.2 = ((bf16[2,2,16,5,1024]{4,1,3,0,2:T(2,128)(2,1)}), bf16[2,2,16,5,1024]{4,1,3,0,2:T(2,128)(2,1)S(1)}, u32[]{:S(2)}, u32[]{:S(2)}) async-start(bf16[2,2,16,5,1024]{4,1,3,0,2:T(2,128)(2,1)} %copy.109), calls=%async_computation.2 | async-start | bytes 1310720 | tf_op jit(solution)/shard_map/all_to_all | solution.py:33
  281.6 2.4 copy-start.4
  285.0 18.2 %collective-permute-start.6 = (bf16[2,1,16,5,1024]{4,3,2,1,0:T(8,128)(2,1)S(1)}, bf16[2,1,16,5,1024]{4,3,2,1,0:T(8,128)(2,1)S(1)}, u32[]{:S(2)}, u32[]{:S(2)}) collective-permute-start(bf16[2,1,16,5,1024]{4,3,2,1,0:T(8,128)(2,1)S(1)} %get-tuple-element.17), channel_id=1, source_target_pairs={{0,32},{32,0},{1,33},{33,1},{2,34},{34,2},{3,35},{35,3},{4,36},{36... | collective-permute-start | bytes 983048 | tf_op jit(solution)/shard_map/ppermute | solution.py:17
  303.4 3.8 %collective-permute-start.7 = (bf16[1,2,16,5,1024]{4,3,2,1,0:T(8,128)(2,1)S(1)}, bf16[1,2,16,5,1024]{4,3,2,1,0:T(8,128)(2,1)S(1)}, u32[]{:S(2)}, u32[]{:S(2)}) collective-permute-start(bf16[1,2,16,5,1024]{4,3,2,1,0:T(8,128)(2,1)S(1)} %get-tuple-element.15), channel_id=1, source_target_pairs={{0,1},{1,0},{2,3},{3,2},{4,5},{5,4},{6,7},{7,6},{8,9},{9,8},{10,11... | collective-permute-start | bytes 983048 | tf_op jit(solution)/shard_map/ppermute | solution.py:17
  313.1 41.7 %all-to-all-start.3 = ((bf16[2,2,16,5,1024]{4,1,3,0,2:T(2,128)(2,1)}), bf16[2,2,16,5,1024]{4,1,3,0,2:T(2,128)(2,1)S(1)}, u32[]{:S(2)}, u32[]{:S(2)}) async-start(bf16[2,2,16,5,1024]{4,1,3,0,2:T(2,128)(2,1)} %copy.113), calls=%async_computation.3 | async-start | bytes 1310720 | tf_op jit(solution)/shard_map/all_to_all | solution.py:37
  322.1 11.1 %collective-permute-start.4 = (bf16[2,1,16,5,1024]{4,2,3,1,0:T(8,128)(2,1)S(1)}, bf16[2,1,16,5,1024]{4,2,3,1,0:T(8,128)(2,1)S(1)}, u32[]{:S(2)}, u32[]{:S(2)}) collective-permute-start(bf16[2,1,16,5,1024]{4,2,3,1,0:T(8,128)(2,1)S(1)} %copy.110), channel_id=1, source_target_pairs={{0,32},{32,0},{1,33},{33,1},{2,34},{34,2},{3,35},{35,3},{4,36},{36... | collective-permute-start | bytes 983048 | tf_op jit(solution)/shard_map/ppermute | solution.py:17
  335.1 20.2 %collective-permute-start.5 = (bf16[1,2,16,5,1024]{4,1,3,0,2:T(2,128)(2,1)S(1)}, bf16[1,2,16,5,1024]{4,1,3,0,2:T(2,128)(2,1)S(1)}, u32[]{:S(2)}, u32[]{:S(2)}) collective-permute-start(bf16[1,2,16,5,1024]{4,1,3,0,2:T(2,128)(2,1)S(1)} %get-tuple-element.7), channel_id=1, source_target_pairs={{0,1},{1,0},{2,3},{3,2},{4,5},{5,4},{6,7},{7,6},{8,9},{9,8},{10,11... | collective-permute-start | bytes 983048 | tf_op jit(solution)/shard_map/ppermute | solution.py:17
  356.4 5.5 %copy-start.1 = (bf16[128,2048]{1,0:T(8,128)(2,1)S(1)}, bf16[128,2048]{1,0:T(8,128)(2,1)}, u32[]{:S(2)}) copy-start(bf16[128,2048]{1,0:T(8,128)(2,1)} %param.7) | copy-start | bytes 1572868
Sparse Core Ops, SparseCore 0:
  11.2 82.2 all-gather.3
  96.7 79.6 all-gather.5
  179.5 77.0 all-gather.7
  264.5 97.3 reduce-scatter.1
where the time goes:
time: 369 us; the launch traced here: 368 us
  waiting for transfers between devices  226 us (61%)
  starting transfers between devices  62 us (17%)
  local copies, waits for them, and re-layouts  30.3 us (8%)
  matrix products  23.4 us (6%)
  between operations  14.3 us (4%)
  other arithmetic  11.9 us (3%)
    all_gather x1, waiting for transfers between devices, body(): w_gate = lax.all_gather(gate_weight, 'dp', axis=1, tiled=True)[0]  76.2 us
    all_to_all x2, waiting for transfers between devices, forward_move(): x = lax.all_to_all(x, 'z', 2, 2, tiled=True)  75.8 us
    ppermute x8, waiting for transfers between devices, swap_half(): got = lax.ppermute(go, axis_name, SWAP)  45.1 us
    all_to_all x2, waiting for transfers between devices, backward_move(): x = lax.all_to_all(x, 'z', 2, 2, tiled=True)  21.7 us
    all_to_all x2, starting transfers between devices, forward_move(): x = lax.all_to_all(x, 'z', 2, 2, tiled=True)  21.5 us
    all_to_all x2, starting transfers between devices, backward_move(): x = lax.all_to_all(x, 'z', 2, 2, tiled=True)  20.2 us
    ppermute x8, starting transfers between devices, swap_half(): got = lax.ppermute(go, axis_name, SWAP)  20.1 us
    concatenate x7, other arithmetic, swap_half(): return jnp.concatenate([stay, got], dim)  9.26 us
  transfers between devices with their start and end apart: 16, of which 13 were waited for; matrix products, arithmetic and copies ran while one was open for 16% of the time, Pallas kernels for 0%

commit v1 on v0

--- a/solution.py
+++ b/solution.py
@@ -45,9 +45,10 @@
     expert_count = n_ylo * n_z * n_core
     capacity = CAP
     positions = expert_count * capacity
-    w_gate = lax.all_gather(gate_weight, "dp", axis=1, tiled=True)[0]
-    w_up = lax.all_gather(up_weight, "dp", axis=1, tiled=True)[0]
-    w_down = lax.all_gather(down_weight, "dp", axis=1, tiled=True)[0]
+    stacked = lax.all_gather(
+        jnp.concatenate([gate_weight, up_weight, down_weight], 0), "dp", axis=1, tiled=True
+    )
+    w_gate, w_up, w_down = stacked[0], stacked[1], stacked[2]
     flat_ids = expert_ids.reshape(-1)
     onehot = (flat_ids[:, None] == jnp.arange(expert_count, dtype=jnp.int32)[None, :]).astype(jnp.int32)
     earlier = jnp.cumsum(onehot, axis=0) - onehot

time: 369 us -> 288 us (0.78)
  waiting for transfers between devices: 226 us -> 146 us
    all_gather x3 -> x1, waiting for transfers between devices: 78.1 us -> 0.01 us  [body(): lax.all_gather(jnp.concatenate([gate_weight, up_weight, down_weight], 0),...]
    all_to_all x2, starting transfers between devices: 20.2 us -> 16.4 us  [backward_move(): x = lax.all_to_all(x, 'z', 2, 2, tiled=True)]
  transfers between devices with their start and end apart: 16 -> 14, of which waited for: 13 -> 11; matrix products, arithmetic and copies ran while one was open for 16% -> 18% of each run, Pallas kernels for 0% -> 0%
where the time goes in v1:
time: 288 us; the launch traced here: 287 us
  waiting for transfers between devices  146 us (51%)
  starting transfers between devices  60.1 us (21%)
  local copies, waits for them, and re-layouts  29.5 us (10%)
  matrix products  23.4 us (8%)
  between operations  14.6 us (5%)
  other arithmetic  13.7 us (5%)
    all_to_all x2, waiting for transfers between devices, forward_move(): x = lax.all_to_all(x, 'z', 2, 2, tiled=True)  73.4 us
    ppermute x8, waiting for transfers between devices, swap_half(): got = lax.ppermute(go, axis_name, SWAP)  48.2 us
    ppermute x8, starting transfers between devices, swap_half(): got = lax.ppermute(go, axis_name, SWAP)  22.1 us
    all_to_all x2, waiting for transfers between devices, backward_move(): x = lax.all_to_all(x, 'z', 2, 2, tiled=True)  21.7 us
    all_to_all x2, starting transfers between devices, forward_move(): x = lax.all_to_all(x, 'z', 2, 2, tiled=True)  21.5 us
    all_to_all x2, starting transfers between devices, backward_move(): x = lax.all_to_all(x, 'z', 2, 2, tiled=True)  16.4 us
    concatenate x7, other arithmetic, swap_half(): return jnp.concatenate([stay, got], dim)  9.26 us
    concatenate x5, local copies, waits for them, and re-layouts, swap_half(): return jnp.concatenate([stay, got], dim)  6.55 us
  transfers between devices with their start and end apart: 14, of which 11 were waited for; matrix products, arithmetic and copies ran while one was open for 18% of the time, Pallas kernels for 0%

profile of v1, /device:TPU:6, one launch (start us, length us, event | category | flops | bytes accessed | tf_op | source)
XLA Modules:
  0.0 287.2 jit_solution(5074170618172507564)
XLA Ops:
  7.2 2.5 pad_maximum_fusion.3
  10.2 0.6 reduce-window.6
  11.7 0.5 convolution_convert_fusion.1
  12.2 0.6 reshape.143
  12.8 2.6 copy.103
  15.4 15.3 %all-to-all-start.1 = ((bf16[2,2,16,5,2048]{4,1,3,0,2:T(2,128)(2,1)}), bf16[2,2,16,5,2048]{4,1,3,0,2:T(2,128)(2,1)S(1)}, u32[]{:S(2)}, u32[]{:S(2)}) async-start(bf16[2,2,16,5,2048]{4,1,3,0,2:T(2,128)(2,1)} %copy.103), calls=%async_computation.1 | async-start | bytes 2621440 | tf_op jit(solution)/shard_map/all_to_all | solution.py:23
  31.2 0.5 fusion.3
  31.7 1.0 fusion.40
  32.6 1.4 slice.102
  34.0 1.3 copy.97
  35.3 1.9 collective-permute-start
  37.6 2.1 collective-permute-done
  39.6 1.5 copy_dynamic-update-slice_fusion
  41.4 0.4 copy.99
  41.8 3.5 %collective-permute-start.1 = (bf16[2,1,16,5,2048]{4,2,3,1,0:T(8,128)(2,1)S(1)}, bf16[2,1,16,5,2048]{4,2,3,1,0:T(8,128)(2,1)S(1)}, u32[]{:S(2)}, u32[]{:S(2)}) collective-permute-start(bf16[2,1,16,5,2048]{4,2,3,1,0:T(8,128)(2,1)S(1)} %copy.99), channel_id=1, source_target_pairs={{0,32},{32,0},{1,33},{33,1},{2,34},{34,2},{3,35},{35,3},{4,36},{36... | collective-permute-start | bytes 1966088 | tf_op jit(solution)/shard_map/ppermute | solution.py:17
  45.3 18.5 %collective-permute-done.1 = bf16[2,1,16,5,2048]{4,2,3,1,0:T(8,128)(2,1)S(1)} collective-permute-done((bf16[2,1,16,5,2048]{4,2,3,1,0:T(8,128)(2,1)S(1)}, bf16[2,1,16,5,2048]{4,2,3,1,0:T(8,128)(2,1)S(1)}, u32[]{:S(2)}, u32[]{:S(2)}) %collective-permute-start.1) | collective-permute-done | bytes 655392 | tf_op jit(solution)/shard_map/ppermute | solution.py:17
  63.7 0.4 copy.100
  64.1 0.5 pad_maximum_fusion
  64.6 2.6 copy.101
  67.2 26.4 %all-to-all-done.1 = bf16[2,2,16,5,2048]{4,1,3,0,2:T(2,128)(2,1)S(1)} async-done(((bf16[2,2,16,5,2048]{4,1,3,0,2:T(2,128)(2,1)}), bf16[2,2,16,5,2048]{4,1,3,0,2:T(2,128)(2,1)S(1)}, u32[]{:S(2)}, u32[]{:S(2)}) %all-to-all-start.1) | async-done | bytes 1310752 | tf_op jit(solution)/shard_map/all_to_all | solution.py:23
  93.6 6.2 %all-to-all-start = ((bf16[2,2,16,5,2048]{4,1,3,0,2:T(2,128)(2,1)}), bf16[2,2,16,5,2048]{4,1,3,0,2:T(2,128)(2,1)S(1)}, u32[]{:S(2)}, u32[]{:S(2)}) async-start(bf16[2,2,16,5,2048]{4,1,3,0,2:T(2,128)(2,1)} %copy.101), calls=%async_computation | async-start | bytes 2621440 | tf_op jit(solution)/shard_map/all_to_all | solution.py:27
  99.9 0.9 fusion.39
  101.0 2.1 collective-permute-start.2
  103.1 1.9 collective-permute-done.2
  105.0 0.7 copy.105
  105.7 3.2 %slice_maximum_fusion = (bf16[2,1,16,5,2048]{4,1,3,0,2:T(2,128)(2,1)}, bf16[2,1,16,5,2048]{4,1,3,0,2:T(2,128)(2,1)S(1)}) fusion(bf16[1,2,16,5,2048]{4,1,3,0,2:T(2,128)(2,1)S(1)} %copy.105, bf16[1,2,16,5,2048]{4,1,3,0,2:T(2,128)(2,1)S(1)} %get-tuple-element.10), kind=kLoop, calls=%fused_computation.24 | loop fusion | flops 2621440 | bytes 2621440 | tf_op jit(solution)/shard_map/concatenate | solution.py:18
  108.8 1.5 copy.106
  110.4 3.5 %collective-permute-start.3 = (bf16[2,1,16,5,2048]{4,2,3,1,0:T(8,128)(2,1)}, bf16[2,1,16,5,2048]{4,2,3,1,0:T(8,128)(2,1)}, u32[]{:S(2)}, u32[]{:S(2)}) collective-permute-start(bf16[2,1,16,5,2048]{4,2,3,1,0:T(8,128)(2,1)} %copy.106), channel_id=1, source_target_pairs={{0,32},{32,0},{1,33},{33,1},{2,34},{34,2},{3,35},{35,3},{4,36},{36... | collective-permute-start | bytes 1966088 | tf_op jit(solution)/shard_map/ppermute | solution.py:17
  113.8 46.9 %all-to-all-done = bf16[2,2,16,5,2048]{4,1,3,0,2:T(2,128)(2,1)S(1)} async-done(((bf16[2,2,16,5,2048]{4,1,3,0,2:T(2,128)(2,1)}), bf16[2,2,16,5,2048]{4,1,3,0,2:T(2,128)(2,1)S(1)}, u32[]{:S(2)}, u32[]{:S(2)}) %all-to-all-start) | async-done | bytes 1310752 | tf_op jit(solution)/shard_map/all_to_all | solution.py:27
  160.8 0.6 copy.102
  161.4 0.6 reshape.142
  162.1 2.9 %copy.107 = bf16[2,1,16,5,2048]{4,1,3,0,2:T(2,128)(2,1)S(1)} copy(bf16[2,1,16,5,2048]{4,2,3,1,0:T(8,128)(2,1)} %collective-permute-done.3) | data formatting | bytes 1310720 | tf_op jit(solution)/shard_map/ppermute | solution.py:17
  165.0 3.0 %pad_maximum_fusion.2 = bf16[2,2,16,5,2048]{4,1,3,0,2:T(2,128)(2,1)S(1)} fusion(bf16[2,1,16,5,2048]{4,1,3,0,2:T(2,128)(2,1)S(1)} %copy.107, bf16[2,1,16,5,2048]{4,1,3,0,2:T(2,128)(2,1)S(1)} %copy-done.2), kind=kLoop, calls=%fused_computation.25 | loop fusion | flops 2621440 | bytes 2621440 | tf_op jit(solution)/shard_map/concatenate | solution.py:18
  168.0 0.6 copy.108
  168.7 1.4 reshape.144
  170.1 3.2 %fusion.2 = f32[320,768]{1,0:T(8,128)S(1)} fusion(bf16[320,2048]{1,0:T(8,128)(2,1)S(1)} %reshape.142, bf16[3,2048,768]{2,1,0:T(8,128)(2,1)} %all-gather.2.cloned.1.call-done), kind=kOutput, calls=%fused_computation.6 | convolution fusion | flops 1006632960 | bytes 5439488 | tf_op jit(solution)/shard_map/dot_general | solution.py:79
  173.3 3.1 %fusion.1 = f32[320,768]{1,0:T(8,128)S(1)} fusion(bf16[320,2048]{1,0:T(8,128)(2,1)S(1)} %copy-done.5, bf16[3,2048,768]{2,1,0:T(8,128)(2,1)} %all-gather.2.cloned.1.call-done), kind=kOutput, calls=%fused_computation.4 | convolution fusion | flops 1006632960 | bytes 5439488 | tf_op jit(solution)/shard_map/dot_general | solution.py:75
  176.3 3.5 %multiply_convert_fusion.2 = (bf16[320,768]{1,0:T(8,128)(2,1)S(1)}, bf16[320,768]{1,0:T(8,128)(2,1)S(1)}, f32[320,768]{1,0:T(8,128)S(1)}) fusion(f32[320,768]{1,0:T(8,128)S(1)} %fusion.2, f32[320,768]{1,0:T(8,128)S(1)} %fusion.1, bf16[320,2048]{1,0:T(8,128)(2,1)S(1)} %copy-done.5, bf16[3,2048,768]{2,1,0:T(8,128)(2,1)} %all-gather.2.cloned.1.call-done), kind=kOutput, calls=%fused_computation.35 | convolution fusion | flops 1009827840 | bytes 8388608 | tf_op jit(solution)/shard_map/dot_general | solution.py:74
  179.8 3.6 %convolution_convert_fusion = bf16[2048,768]{1,0:T(8,128)(2,1)} fusion(bf16[320,2048]{1,0:T(8,128)(2,1)S(1)} %copy-done.4, f32[320,768]{1,0:T(8,128)S(1)} %fusion.1, f32[320,768]{1,0:T(8,128)S(1)} %get-tuple-element.20), kind=kOutput, calls=%fused_computation | convolution fusion | flops 1009680384 | bytes 6422528 | tf_op jit(solution)/shard_map/dot_general | solution.py:104
  183.5 2.1 fusion.6
  185.6 2.1 fusion.11
  188.0 1.7 copy.109
  189.6 8.4 %all-to-all-start.2 = ((bf16[2,2,16,5,1024]{4,1,3,0,2:T(2,128)(2,1)}), bf16[2,2,16,5,1024]{4,1,3,0,2:T(2,128)(2,1)S(1)}, u32[]{:S(2)}, u32[]{:S(2)}) async-start(bf16[2,2,16,5,1024]{4,1,3,0,2:T(2,128)(2,1)} %copy.109), calls=%async_computation.2 | async-start | bytes 1310720 | tf_op jit(solution)/shard_map/all_to_all | solution.py:33
  198.1 2.1 fusion.4
  200.3 2.1 fusion.10
  202.7 3.5 %collective-permute-start.6 = (bf16[2,1,16,5,1024]{4,3,2,1,0:T(8,128)(2,1)S(1)}, bf16[2,1,16,5,1024]{4,3,2,1,0:T(8,128)(2,1)S(1)}, u32[]{:S(2)}, u32[]{:S(2)}) collective-permute-start(bf16[2,1,16,5,1024]{4,3,2,1,0:T(8,128)(2,1)S(1)} %get-tuple-element.17), channel_id=1, source_target_pairs={{0,32},{32,0},{1,33},{33,1},{2,34},{34,2},{3,35},{35,3},{4,36},{36... | collective-permute-start | bytes 983048 | tf_op jit(solution)/shard_map/ppermute | solution.py:17
  206.2 16.4 %collective-permute-done.6 = bf16[2,1,16,5,1024]{4,3,2,1,0:T(8,128)(2,1)S(1)} collective-permute-done((bf16[2,1,16,5,1024]{4,3,2,1,0:T(8,128)(2,1)S(1)}, bf16[2,1,16,5,1024]{4,3,2,1,0:T(8,128)(2,1)S(1)}, u32[]{:S(2)}, u32[]{:S(2)}) %collective-permute-start.6) | collective-permute-done | bytes 327712 | tf_op jit(solution)/shard_map/ppermute | solution.py:17
  222.8 1.9 collective-permute-start.7
  224.8 1.9 collective-permute-done.7
  226.9 1.6 copy.113
  228.5 3.8 %all-to-all-done.2 = bf16[2,2,16,5,1024]{4,1,3,0,2:T(2,128)(2,1)S(1)} async-done(((bf16[2,2,16,5,1024]{4,1,3,0,2:T(2,128)(2,1)}), bf16[2,2,16,5,1024]{4,1,3,0,2:T(2,128)(2,1)S(1)}, u32[]{:S(2)}, u32[]{:S(2)}) %all-to-all-start.2) | async-done | bytes 655392 | tf_op jit(solution)/shard_map/all_to_all | solution.py:33
  232.3 8.0 %all-to-all-start.3 = ((bf16[2,2,16,5,1024]{4,1,3,0,2:T(2,128)(2,1)}), bf16[2,2,16,5,1024]{4,1,3,0,2:T(2,128)(2,1)S(1)}, u32[]{:S(2)}, u32[]{:S(2)}) async-start(bf16[2,2,16,5,1024]{4,1,3,0,2:T(2,128)(2,1)} %copy.113), calls=%async_computation.3 | async-start | bytes 1310720 | tf_op jit(solution)/shard_map/all_to_all | solution.py:37
  240.2 0.9 fusion.42
  241.3 3.8 %collective-permute-start.4 = (bf16[2,1,16,5,1024]{4,2,3,1,0:T(8,128)(2,1)S(1)}, bf16[2,1,16,5,1024]{4,2,3,1,0:T(8,128)(2,1)S(1)}, u32[]{:S(2)}, u32[]{:S(2)}) collective-permute-start(bf16[2,1,16,5,1024]{4,2,3,1,0:T(8,128)(2,1)S(1)} %copy.110), channel_id=1, source_target_pairs={{0,32},{32,0},{1,33},{33,1},{2,34},{34,2},{3,35},{35,3},{4,36},{36... | collective-permute-start | bytes 983048 | tf_op jit(solution)/shard_map/ppermute | solution.py:17
  245.2 7.5 %collective-permute-done.4 = bf16[2,1,16,5,1024]{4,2,3,1,0:T(8,128)(2,1)S(1)} collective-permute-done((bf16[2,1,16,5,1024]{4,2,3,1,0:T(8,128)(2,1)S(1)}, bf16[2,1,16,5,1024]{4,2,3,1,0:T(8,128)(2,1)S(1)}, u32[]{:S(2)}, u32[]{:S(2)}) %collective-permute-start.4) | collective-permute-done | bytes 327712 | tf_op jit(solution)/shard_map/ppermute | solution.py:17
  252.7 0.5 copy.111
  253.2 1.4 fusion.14
  254.6 1.9 collective-permute-start.5
  256.5 18.0 %all-to-all-done.3 = bf16[2,2,16,5,1024]{4,1,3,0,2:T(2,128)(2,1)S(1)} async-done(((bf16[2,2,16,5,1024]{4,1,3,0,2:T(2,128)(2,1)}), bf16[2,2,16,5,1024]{4,1,3,0,2:T(2,128)(2,1)S(1)}, u32[]{:S(2)}, u32[]{:S(2)}) %all-to-all-start.3) | async-done | bytes 655392 | tf_op jit(solution)/shard_map/all_to_all | solution.py:37
  275.0 0.8 pad_maximum_fusion.5
  276.4 0.3 convolution_convert_fusion.2
  276.7 0.3 convolution_convert_fusion.3
  277.0 0.8 pad_maximum_fusion.7
  277.9 2.5 reduce-scatter.2.cloned.1.call-done
  (57 shorter events, 4.9 us)
Async XLA Ops:
  7.2 4.5 %copy-start = (bf16[128,2048]{1,0:T(8,128)(2,1)S(1)}, bf16[128,2048]{1,0:T(8,128)(2,1)}, u32[]{:S(2)}) copy-start(bf16[128,2048]{1,0:T(8,128)(2,1)} %param.7) | copy-start | bytes 1572868
  7.2 2.6 copy-start.7
  7.2 162.9 %all-gather.2.cloned.1.call-start = ((), (), s32[]{:S(2)}) async-start(), calls=%async_computation.5 | async-start | bytes 10616832 | tf_op jit(solution)/shard_map/all_gather | solution.py:48
  15.4 15.3 %copy-start.8 = (f32[128,2]{0,1:T(2,128)S(1)}, f32[128,2]{0,1:T(2,128)}, u32[]{:S(2)}) copy-start(f32[128,2]{0,1:T(2,128)} %param.9) | copy-start | bytes 3076
  15.4 15.8 %copy-start.6 = (bf16[128,2048]{1,0:T(8,128)(2,1)S(1)}, bf16[128,2048]{1,0:T(8,128)(2,1)}, u32[]{:S(2)}) copy-start(bf16[128,2048]{1,0:T(8,128)(2,1)} %param.8) | copy-start | bytes 1572868
  15.4 78.2 %all-to-all-start.1 = ((bf16[2,2,16,5,2048]{4,1,3,0,2:T(2,128)(2,1)}), bf16[2,2,16,5,2048]{4,1,3,0,2:T(2,128)(2,1)S(1)}, u32[]{:S(2)}, u32[]{:S(2)}) async-start(bf16[2,2,16,5,2048]{4,1,3,0,2:T(2,128)(2,1)} %copy.103), calls=%async_computation.1 | async-start | bytes 2621440 | tf_op jit(solution)/shard_map/all_to_all | solution.py:23
  35.3 4.3 %collective-permute-start = (bf16[1,2,16,5,2048]{4,2,3,1,0:T(8,128)(2,1)}, bf16[1,2,16,5,2048]{4,2,3,1,0:T(8,128)(2,1)}, u32[]{:S(2)}, u32[]{:S(2)}) collective-permute-start(bf16[1,2,16,5,2048]{4,2,3,1,0:T(8,128)(2,1)} %copy.97), channel_id=1, source_target_pairs={{0,1},{1,0},{2,3},{3,2},{4,5},{5,4},{6,7},{7,6},{8,9},{9,8},{10,11... | collective-permute-start | bytes 1966088 | tf_op jit(solution)/shard_map/ppermute | solution.py:17
  41.8 21.9 %collective-permute-start.1 = (bf16[2,1,16,5,2048]{4,2,3,1,0:T(8,128)(2,1)S(1)}, bf16[2,1,16,5,2048]{4,2,3,1,0:T(8,128)(2,1)S(1)}, u32[]{:S(2)}, u32[]{:S(2)}) collective-permute-start(bf16[2,1,16,5,2048]{4,2,3,1,0:T(8,128)(2,1)S(1)} %copy.99), channel_id=1, source_target_pairs={{0,32},{32,0},{1,33},{33,1},{2,34},{34,2},{3,35},{35,3},{4,36},{36... | collective-permute-start | bytes 1966088 | tf_op jit(solution)/shard_map/ppermute | solution.py:17
  93.6 67.2 %all-to-all-start = ((bf16[2,2,16,5,2048]{4,1,3,0,2:T(2,128)(2,1)}), bf16[2,2,16,5,2048]{4,1,3,0,2:T(2,128)(2,1)S(1)}, u32[]{:S(2)}, u32[]{:S(2)}) async-start(bf16[2,2,16,5,2048]{4,1,3,0,2:T(2,128)(2,1)} %copy.101), calls=%async_computation | async-start | bytes 2621440 | tf_op jit(solution)/shard_map/all_to_all | solution.py:27
  99.8 180.5 %reduce-scatter.2.cloned.1.call-start = ((), (), s32[]{:S(2)}) async-start(), calls=%async_computation.6 | async-start | bytes 3538944 | tf_op jit(solution)/shard_map/reduce_scatter | solution.py:103
  101.0 4.0 %collective-permute-start.2 = (bf16[1,2,16,5,2048]{4,2,3,1,0:T(8,128)(2,1)S(1)}, bf16[1,2,16,5,2048]{4,2,3,1,0:T(8,128)(2,1)S(1)}, u32[]{:S(2)}, u32[]{:S(2)}) collective-permute-start(bf16[1,2,16,5,2048]{4,2,3,1,0:T(8,128)(2,1)S(1)} %copy.104), channel_id=1, source_target_pairs={{0,1},{1,0},{2,3},{3,2},{4,5},{5,4},{6,7},{7,6},{8,9},{9,8},{10,11... | collective-permute-start | bytes 1966088 | tf_op jit(solution)/shard_map/ppermute | solution.py:17
  110.4 51.7 %collective-permute-start.3 = (bf16[2,1,16,5,2048]{4,2,3,1,0:T(8,128)(2,1)}, bf16[2,1,16,5,2048]{4,2,3,1,0:T(8,128)(2,1)}, u32[]{:S(2)}, u32[]{:S(2)}) collective-permute-start(bf16[2,1,16,5,2048]{4,2,3,1,0:T(8,128)(2,1)} %copy.106), channel_id=1, source_target_pairs={{0,32},{32,0},{1,33},{33,1},{2,34},{34,2},{3,35},{35,3},{4,36},{36... | collective-permute-start | bytes 1966088 | tf_op jit(solution)/shard_map/ppermute | solution.py:17
  162.0 8.1 %copy-start.3 = (bf16[320,2048]{1,0:T(8,128)(2,1)}, bf16[320,2048]{1,0:T(8,128)(2,1)S(1)}, u32[]{:S(2)}) copy-start(bf16[320,2048]{1,0:T(8,128)(2,1)S(1)} %reshape.142) | copy-start | bytes 3932164
  162.0 3.0 %copy-start.2 = (bf16[2,1,16,5,2048]{4,1,3,0,2:T(2,128)(2,1)S(1)}, bf16[2,1,16,5,2048]{4,1,3,0,2:T(2,128)(2,1)}, u32[]{:S(2)}) copy-start(bf16[2,1,16,5,2048]{4,1,3,0,2:T(2,128)(2,1)} %get-tuple-element.8) | copy-start | bytes 1966084
  170.1 3.2 %copy-start.5 = (bf16[320,2048]{1,0:T(8,128)(2,1)S(1)}, bf16[320,2048]{1,0:T(8,128)(2,1)}, u32[]{:S(2)}) copy-start(bf16[320,2048]{1,0:T(8,128)(2,1)} %reshape.144) | copy-start | bytes 3932164
  176.3 3.5 %copy-start.4 = (bf16[320,2048]{1,0:T(8,128)(2,1)S(1)}, bf16[320,2048]{1,0:T(8,128)(2,1)}, u32[]{:S(2)}) copy-start(bf16[320,2048]{1,0:T(8,128)(2,1)} %copy-done.3) | copy-start | bytes 3932164
  189.6 42.6 %all-to-all-start.2 = ((bf16[2,2,16,5,1024]{4,1,3,0,2:T(2,128)(2,1)}), bf16[2,2,16,5,1024]{4,1,3,0,2:T(2,128)(2,1)S(1)}, u32[]{:S(2)}, u32[]{:S(2)}) async-start(bf16[2,2,16,5,1024]{4,1,3,0,2:T(2,128)(2,1)} %copy.109), calls=%async_computation.2 | async-start | bytes 1310720 | tf_op jit(solution)/shard_map/all_to_all | solution.py:33
  202.7 19.9 %collective-permute-start.6 = (bf16[2,1,16,5,1024]{4,3,2,1,0:T(8,128)(2,1)S(1)}, bf16[2,1,16,5,1024]{4,3,2,1,0:T(8,128)(2,1)S(1)}, u32[]{:S(2)}, u32[]{:S(2)}) collective-permute-start(bf16[2,1,16,5,1024]{4,3,2,1,0:T(8,128)(2,1)S(1)} %get-tuple-element.17), channel_id=1, source_target_pairs={{0,32},{32,0},{1,33},{33,1},{2,34},{34,2},{3,35},{35,3},{4,36},{36... | collective-permute-start | bytes 983048 | tf_op jit(solution)/shard_map/ppermute | solution.py:17
  222.8 3.8 %collective-permute-start.7 = (bf16[1,2,16,5,1024]{4,3,2,1,0:T(8,128)(2,1)S(1)}, bf16[1,2,16,5,1024]{4,3,2,1,0:T(8,128)(2,1)S(1)}, u32[]{:S(2)}, u32[]{:S(2)}) collective-permute-start(bf16[1,2,16,5,1024]{4,3,2,1,0:T(8,128)(2,1)S(1)} %get-tuple-element.15), channel_id=1, source_target_pairs={{0,1},{1,0},{2,3},{3,2},{4,5},{5,4},{6,7},{7,6},{8,9},{9,8},{10,11... | collective-permute-start | bytes 983048 | tf_op jit(solution)/shard_map/ppermute | solution.py:17
  232.3 42.2 %all-to-all-start.3 = ((bf16[2,2,16,5,1024]{4,1,3,0,2:T(2,128)(2,1)}), bf16[2,2,16,5,1024]{4,1,3,0,2:T(2,128)(2,1)S(1)}, u32[]{:S(2)}, u32[]{:S(2)}) async-start(bf16[2,2,16,5,1024]{4,1,3,0,2:T(2,128)(2,1)} %copy.113), calls=%async_computation.3 | async-start | bytes 1310720 | tf_op jit(solution)/shard_map/all_to_all | solution.py:37
  241.3 11.4 %collective-permute-start.4 = (bf16[2,1,16,5,1024]{4,2,3,1,0:T(8,128)(2,1)S(1)}, bf16[2,1,16,5,1024]{4,2,3,1,0:T(8,128)(2,1)S(1)}, u32[]{:S(2)}, u32[]{:S(2)}) collective-permute-start(bf16[2,1,16,5,1024]{4,2,3,1,0:T(8,128)(2,1)S(1)} %copy.110), channel_id=1, source_target_pairs={{0,32},{32,0},{1,33},{33,1},{2,34},{34,2},{3,35},{35,3},{4,36},{36... | collective-permute-start | bytes 983048 | tf_op jit(solution)/shard_map/ppermute | solution.py:17
  254.6 20.4 %collective-permute-start.5 = (bf16[1,2,16,5,1024]{4,1,3,0,2:T(2,128)(2,1)S(1)}, bf16[1,2,16,5,1024]{4,1,3,0,2:T(2,128)(2,1)S(1)}, u32[]{:S(2)}, u32[]{:S(2)}) collective-permute-start(bf16[1,2,16,5,1024]{4,1,3,0,2:T(2,128)(2,1)S(1)} %get-tuple-element.7), channel_id=1, source_target_pairs={{0,1},{1,0},{2,3},{3,2},{4,5},{5,4},{6,7},{7,6},{8,9},{9,8},{10,11... | collective-permute-start | bytes 983048 | tf_op jit(solution)/shard_map/ppermute | solution.py:17
  276.1 4.3 %copy-start.1 = (bf16[128,2048]{1,0:T(8,128)(2,1)S(1)}, bf16[128,2048]{1,0:T(8,128)(2,1)}, u32[]{:S(2)}) copy-start(bf16[128,2048]{1,0:T(8,128)(2,1)} %param.7) | copy-start | bytes 1572868
Sparse Core Ops, SparseCore 0:
  11.2 153.5 all-gather.1
  183.6 96.6 reduce-scatter.1

commit v2 on v1

--- a/solution.py
+++ b/solution.py
@@ -68,7 +68,7 @@
     row_send = jnp.dot(picker, tokens, preferred_element_type=jnp.float32).astype(jnp.bfloat16)
     picked_grad = jnp.dot(picker, out_grad, preferred_element_type=jnp.float32)
     grad_send = (slot_weight[:, None] * picked_grad).astype(jnp.bfloat16)
-    block = (n_core, n_ylo, n_z, capacity, width)
+    block = (n_core, n_ylo, n_z * capacity, width)
     rows_in = forward_move(row_send.reshape(block), True).reshape(positions, width)
     grads_in = forward_move(grad_send.reshape(block), False).reshape(positions, width)
     gate_pre = jnp.dot(rows_in, w_gate, preferred_element_type=jnp.float32)

time: 288 us -> 289 us (level)
  waiting for transfers between devices: 146 us -> 167 us
  local copies, waits for them, and re-layouts: 29.5 us -> 15.2 us
  other arithmetic: 13.7 us -> 7.24 us
    all_gather x1, waiting for transfers between devices: 0.01 us -> 7.29 us  [body(): lax.all_gather(jnp.concatenate([gate_weight, up_weight, down_weight], 0),...]
    concatenate x7 -> x6, other arithmetic: 9.26 us -> 2.78 us  [swap_half(): return jnp.concatenate([stay, got], dim)]
    all_to_all x2, waiting for transfers between devices: 21.7 us -> 28.1 us  [backward_move(): x = lax.all_to_all(x, 'z', 2, 2, tiled=True)]
    ppermute x4 -> x0, local copies, waits for them, and re-layouts: 4.5 us -> none  [swap_half(): got = lax.ppermute(go, axis_name, SWAP)]
    slice x7 -> x2, local copies, waits for them, and re-layouts: 5.97 us -> 1.81 us  [swap_half(): go = lax.index_in_dim(x, 1, dim, keepdims=True)]
    all_to_all x2, waiting for transfers between devices: 73.4 us -> 77.3 us  [forward_move(): x = lax.all_to_all(x, 'z', 2, 2, tiled=True)]
    all_to_all x2, starting transfers between devices: 16.4 us -> 19.8 us  [backward_move(): x = lax.all_to_all(x, 'z', 2, 2, tiled=True)]
    concatenate x5 -> x4, local copies, waits for them, and re-layouts: 6.55 us -> 4.04 us  [swap_half(): return jnp.concatenate([stay, got], dim)]
  transfers between devices with their start and end apart: 14 -> 14, of which waited for: 11 -> 12; matrix products, arithmetic and copies ran while one was open for 18% -> 10% of each run, Pallas kernels for 0% -> 0%
where the time goes in v2:
time: 289 us
  waiting for transfers between devices  167 us (58%)
  starting transfers between devices  61.4 us (21%)
  matrix products  23.5 us (8%)
  local copies, waits for them, and re-layouts  15.2 us (5%)
  between operations  14.5 us (5%)
  other arithmetic  7.24 us (3%)
    all_to_all x2, waiting for transfers between devices, forward_move(): x = lax.all_to_all(x, 'z', 2, 2, tiled=True)  77.3 us
    ppermute x8, waiting for transfers between devices, swap_half(): got = lax.ppermute(go, axis_name, SWAP)  50.9 us
    all_to_all x2, waiting for transfers between devices, backward_move(): x = lax.all_to_all(x, 'z', 2, 2, tiled=True)  28.1 us
    all_to_all x2, starting transfers between devices, forward_move(): x = lax.all_to_all(x, 'z', 2, 2, tiled=True)  21.5 us
    ppermute x8, starting transfers between devices, swap_half(): got = lax.ppermute(go, axis_name, SWAP)  20 us
    all_to_all x2, starting transfers between devices, backward_move(): x = lax.all_to_all(x, 'z', 2, 2, tiled=True)  19.8 us
    all_gather x1, waiting for transfers between devices, body(): lax.all_gather(jnp.concatenate([gate_weight, up_weight, down_weight], 0),...  7.29 us
  transfers between devices with their start and end apart: 14, of which 12 were waited for; matrix products, arithmetic and copies ran while one was open for 10% of the time, Pallas kernels for 0%

profile of v2, /device:TPU:6, one launch (start us, length us, event | category | flops | bytes accessed | tf_op | source)
XLA Modules:
  0.0 288.5 jit_solution(8477086625098563129)
XLA Ops:
  7.2 2.5 pad_maximum_fusion.2
  9.8 0.1 copy.91
  9.9 0.1 eq.48
  10.0 0.1 eq.52
  10.2 0.6 reduce-window.6
  10.8 0.2 slice_reduce_fusion
  11.1 0.1 reduce_sum.30
  11.3 0.1 copy.94
  11.4 0.1 fusion.22
  11.7 0.5 convolution_convert_fusion.1
  12.2 2.4 copy.106
  14.6 15.3 %all-to-all-start.1 = ((bf16[2,2,80,2048]{3,1,0,2:T(2,128)(2,1)}), bf16[2,2,80,2048]{3,1,0,2:T(2,128)(2,1)S(1)}, u32[]{:S(2)}, u32[]{:S(2)}) async-start(bf16[2,2,80,2048]{3,1,0,2:T(2,128)(2,1)} %copy.106), calls=%async_computation.1 | async-start | bytes 2621440 | tf_op jit(solution)/shard_map/all_to_all | solution.py:23
  30.1 0.1 broadcast_in_dim.21
  30.3 0.1 select_reduce_fusion
  30.4 0.5 fusion.3
  31.0 1.9 collective-permute-start
  33.0 2.1 collective-permute-done
  35.0 0.1 fusion.13
  35.1 3.5 %collective-permute-start.1 = (bf16[2,1,80,2048]{3,2,1,0:T(8,128)(2,1)S(1)}, bf16[2,1,80,2048]{3,2,1,0:T(8,128)(2,1)S(1)}, u32[]{:S(2)}, u32[]{:S(2)}) collective-permute-start(bf16[2,1,80,2048]{3,2,1,0:T(8,128)(2,1)S(1)} %get-tuple-element.9), channel_id=1, source_target_pairs={{0,32},{32,0},{1,33},{33,1},{2,34},{34,2},{3,35},{35,3},{4,36},{36... | collective-permute-start | bytes 1966088 | tf_op jit(solution)/shard_map/ppermute | solution.py:17
  38.6 25.1 %collective-permute-done.1 = bf16[2,1,80,2048]{3,2,1,0:T(8,128)(2,1)S(1)} collective-permute-done((bf16[2,1,80,2048]{3,2,1,0:T(8,128)(2,1)S(1)}, bf16[2,1,80,2048]{3,2,1,0:T(8,128)(2,1)S(1)}, u32[]{:S(2)}, u32[]{:S(2)}) %collective-permute-start.1) | collective-permute-done | bytes 655392 | tf_op jit(solution)/shard_map/ppermute | solution.py:17
  63.7 0.1 pad_maximum_fusion
  63.9 2.5 copy.104
  66.3 26.5 %all-to-all-done.1 = bf16[2,2,80,2048]{3,1,0,2:T(2,128)(2,1)S(1)} async-done(((bf16[2,2,80,2048]{3,1,0,2:T(2,128)(2,1)}), bf16[2,2,80,2048]{3,1,0,2:T(2,128)(2,1)S(1)}, u32[]{:S(2)}, u32[]{:S(2)}) %all-to-all-start.1) | async-done | bytes 1310752 | tf_op jit(solution)/shard_map/all_to_all | solution.py:23
  92.9 6.2 %all-to-all-start = ((bf16[2,2,80,2048]{3,1,0,2:T(2,128)(2,1)}), bf16[2,2,80,2048]{3,1,0,2:T(2,128)(2,1)S(1)}, u32[]{:S(2)}, u32[]{:S(2)}) async-start(bf16[2,2,80,2048]{3,1,0,2:T(2,128)(2,1)} %copy.104), calls=%async_computation | async-start | bytes 2621440 | tf_op jit(solution)/shard_map/all_to_all | solution.py:27
  99.1 0.9 fusion.39
  100.0 0.2 copy.115
  100.2 1.9 collective-permute-start.2
  102.2 0.2 copy_dynamic-update-slice_fusion
  102.4 1.9 collective-permute-done.2
  104.3 1.1 fusion.38
  105.4 3.8 %collective-permute-start.3 = (bf16[2,1,80,2048]{3,2,1,0:T(8,128)(2,1)}, bf16[2,1,80,2048]{3,2,1,0:T(8,128)(2,1)}, u32[]{:S(2)}, u32[]{:S(2)}) collective-permute-start(bf16[2,1,80,2048]{3,2,1,0:T(8,128)(2,1)} %get-tuple-element.5), channel_id=1, source_target_pairs={{0,32},{32,0},{1,33},{33,1},{2,34},{34,2},{3,35},{35,3},{4,36},{36... | collective-permute-start | bytes 1966088 | tf_op jit(solution)/shard_map/ppermute | solution.py:17
  109.2 50.8 %all-to-all-done = bf16[2,2,80,2048]{3,1,0,2:T(2,128)(2,1)S(1)} async-done(((bf16[2,2,80,2048]{3,1,0,2:T(2,128)(2,1)}), bf16[2,2,80,2048]{3,1,0,2:T(2,128)(2,1)S(1)}, u32[]{:S(2)}, u32[]{:S(2)}) %all-to-all-start) | async-done | bytes 1310752 | tf_op jit(solution)/shard_map/all_to_all | solution.py:27
  160.0 1.8 copy.105
  161.8 2.4 pad_maximum_fusion.1
  164.2 7.3 %all-gather.2.cloned.1.call-done = bf16[3,2048,768]{2,1,0:T(8,128)(2,1)} async-done(((bf16[3,256,768]{2,1,0:T(8,128)(2,1)}), bf16[3,2048,768]{2,1,0:T(8,128)(2,1)}) %all-gather.2.cloned.1.call-update) | async-done | bytes 9437200 | tf_op jit(solution)/shard_map/all_gather | solution.py:48
  171.5 3.2 %fusion.2 = f32[320,768]{1,0:T(8,128)S(1)} fusion(bf16[320,2048]{1,0:T(8,128)(2,1)S(1)} %bitcast.82, bf16[3,2048,768]{2,1,0:T(8,128)(2,1)} %all-gather.2.cloned.1.call-done), kind=kOutput, calls=%fused_computation.6 | convolution fusion | flops 1006632960 | bytes 5439488 | tf_op jit(solution)/shard_map/dot_general | solution.py:79
  174.7 3.1 %fusion.1 = f32[320,768]{1,0:T(8,128)S(1)} fusion(bf16[320,2048]{1,0:T(8,128)(2,1)S(1)} %bitcast.84, bf16[3,2048,768]{2,1,0:T(8,128)(2,1)} %all-gather.2.cloned.1.call-done), kind=kOutput, calls=%fused_computation.4 | convolution fusion | flops 1006632960 | bytes 5439488 | tf_op jit(solution)/shard_map/dot_general | solution.py:75
  177.8 3.4 %multiply_convert_fusion.2 = (bf16[320,768]{1,0:T(8,128)(2,1)S(1)}, bf16[320,768]{1,0:T(8,128)(2,1)S(1)}, f32[320,768]{1,0:T(8,128)S(1)}) fusion(f32[320,768]{1,0:T(8,128)S(1)} %fusion.2, f32[320,768]{1,0:T(8,128)S(1)} %fusion.1, bf16[320,2048]{1,0:T(8,128)(2,1)S(1)} %bitcast.85, bf16[3,2048,768]{2,1,0:T(8,128)(2,1)} %all-gather.2.cloned.1.call-done), kind=kOutput, calls=%fused_computation.31 | convolution fusion | flops 1009827840 | bytes 8388608 | tf_op jit(solution)/shard_map/dot_general | solution.py:74
  181.2 3.6 %convolution_convert_fusion = bf16[2048,768]{1,0:T(8,128)(2,1)} fusion(bf16[320,2048]{1,0:T(8,128)(2,1)S(1)} %bitcast.83, f32[320,768]{1,0:T(8,128)S(1)} %fusion.1, f32[320,768]{1,0:T(8,128)S(1)} %get-tuple-element.20), kind=kOutput, calls=%fused_computation | convolution fusion | flops 1009680384 | bytes 6422528 | tf_op jit(solution)/shard_map/dot_general | solution.py:104
  184.8 2.1 fusion.6
  186.9 2.1 fusion.11
  189.0 1.6 copy.109
  190.6 12.3 %all-to-all-start.2 = ((bf16[2,2,80,1024]{3,1,0,2:T(2,128)(2,1)}), bf16[2,2,80,1024]{3,1,0,2:T(2,128)(2,1)S(1)}, u32[]{:S(2)}, u32[]{:S(2)}) async-start(bf16[2,2,80,1024]{3,1,0,2:T(2,128)(2,1)} %copy.109), calls=%async_computation.2 | async-start | bytes 1310720 | tf_op jit(solution)/shard_map/all_to_all | solution.py:33
  202.9 2.3 fusion.4
  205.2 2.1 fusion.10
  207.4 2.5 collective-permute-start.6
  209.9 12.1 %collective-permute-done.6 = bf16[2,1,80,1024]{3,2,1,0:T(8,128)(2,1)S(1)} collective-permute-done((bf16[2,1,80,1024]{3,2,1,0:T(8,128)(2,1)S(1)}, bf16[2,1,80,1024]{3,2,1,0:T(8,128)(2,1)S(1)}, u32[]{:S(2)}, u32[]{:S(2)}) %collective-permute-start.6) | collective-permute-done | bytes 327712 | tf_op jit(solution)/shard_map/ppermute | solution.py:17
  222.1 1.9 collective-permute-start.7
  224.0 1.6 collective-permute-done.7
  225.7 1.5 copy.112
  227.2 8.8 %all-to-all-done.2 = bf16[2,2,80,1024]{3,1,0,2:T(2,128)(2,1)S(1)} async-done(((bf16[2,2,80,1024]{3,1,0,2:T(2,128)(2,1)}), bf16[2,2,80,1024]{3,1,0,2:T(2,128)(2,1)S(1)}, u32[]{:S(2)}, u32[]{:S(2)}) %all-to-all-start.2) | async-done | bytes 655392 | tf_op jit(solution)/shard_map/all_to_all | solution.py:33
  236.0 7.6 %all-to-all-start.3 = ((bf16[2,2,80,1024]{3,1,0,2:T(2,128)(2,1)}), bf16[2,2,80,1024]{3,1,0,2:T(2,128)(2,1)S(1)}, u32[]{:S(2)}, u32[]{:S(2)}) async-start(bf16[2,2,80,1024]{3,1,0,2:T(2,128)(2,1)} %copy.112), calls=%async_computation.3 | async-start | bytes 1310720 | tf_op jit(solution)/shard_map/all_to_all | solution.py:37
  243.5 0.9 fusion.42
  244.4 0.2 copy.117
  244.6 2.5 collective-permute-start.4
  247.1 0.2 copy_dynamic-update-slice_fusion.1
  247.3 8.1 %collective-permute-done.4 = bf16[2,1,80,1024]{3,2,1,0:T(8,128)(2,1)S(1)} collective-permute-done((bf16[2,1,80,1024]{3,2,1,0:T(8,128)(2,1)S(1)}, bf16[2,1,80,1024]{3,2,1,0:T(8,128)(2,1)S(1)}, u32[]{:S(2)}, u32[]{:S(2)}) %collective-permute-start.4) | collective-permute-done | bytes 327712 | tf_op jit(solution)/shard_map/ppermute | solution.py:17
  255.6 1.9 collective-permute-start.5
  257.5 19.3 %all-to-all-done.3 = bf16[2,2,80,1024]{3,1,0,2:T(2,128)(2,1)S(1)} async-done(((bf16[2,2,80,1024]{3,1,0,2:T(2,128)(2,1)}), bf16[2,2,80,1024]{3,1,0,2:T(2,128)(2,1)S(1)}, u32[]{:S(2)}, u32[]{:S(2)}) %all-to-all-start.3) | async-done | bytes 655392 | tf_op jit(solution)/shard_map/all_to_all | solution.py:37
  276.8 0.2 copy.113
  277.1 0.3 convolution_convert_fusion.2
  277.4 0.3 convolution_convert_fusion.3
  277.7 0.8 pad_maximum_fusion.6
  278.6 3.1 %reduce-scatter.2.cloned.1.call-done = bf16[256,768]{1,0:T(8,128)(2,1)} async-done(((bf16[2048,768]{1,0:T(8,128)(2,1)}), bf16[256,768]{1,0:T(8,128)(2,1)}) %reduce-scatter.2.cloned.1.call-update) | async-done | bytes 393232 | tf_op jit(solution)/shard_map/reduce_scatter | solution.py:103
  (39 shorter events, 1.0 us)
Async XLA Ops:
  7.2 4.5 %copy-start = (bf16[128,2048]{1,0:T(8,128)(2,1)S(1)}, bf16[128,2048]{1,0:T(8,128)(2,1)}, u32[]{:S(2)}) copy-start(bf16[128,2048]{1,0:T(8,128)(2,1)} %param.7) | copy-start | bytes 1572868
  7.2 2.6 copy-start.5
  7.2 164.3 %all-gather.2.cloned.1.call-start = ((), (), s32[]{:S(2)}) async-start(), calls=%async_computation.5 | async-start | bytes 10616832 | tf_op jit(solution)/shard_map/all_gather | solution.py:48
  14.6 15.3 %copy-start.6 = (f32[128,2]{0,1:T(2,128)S(1)}, f32[128,2]{0,1:T(2,128)}, u32[]{:S(2)}) copy-start(f32[128,2]{0,1:T(2,128)} %param.9) | copy-start | bytes 3076
  14.6 15.8 %copy-start.4 = (bf16[128,2048]{1,0:T(8,128)(2,1)S(1)}, bf16[128,2048]{1,0:T(8,128)(2,1)}, u32[]{:S(2)}) copy-start(bf16[128,2048]{1,0:T(8,128)(2,1)} %param.8) | copy-start | bytes 1572868
  14.6 78.2 %all-to-all-start.1 = ((bf16[2,2,80,2048]{3,1,0,2:T(2,128)(2,1)}), bf16[2,2,80,2048]{3,1,0,2:T(2,128)(2,1)S(1)}, u32[]{:S(2)}, u32[]{:S(2)}) async-start(bf16[2,2,80,2048]{3,1,0,2:T(2,128)(2,1)} %copy.106), calls=%async_computation.1 | async-start | bytes 2621440 | tf_op jit(solution)/shard_map/all_to_all | solution.py:23
  31.0 4.0 %collective-permute-start = (bf16[1,2,80,2048]{3,2,1,0:T(8,128)(2,1)S(1)}, bf16[1,2,80,2048]{3,2,1,0:T(8,128)(2,1)S(1)}, u32[]{:S(2)}, u32[]{:S(2)}) collective-permute-start(bf16[1,2,80,2048]{3,2,1,0:T(8,128)(2,1)S(1)} %bitcast.86), channel_id=1, source_target_pairs={{0,1},{1,0},{2,3},{3,2},{4,5},{5,4},{6,7},{7,6},{8,9},{9,8},{10,11... | collective-permute-start | bytes 1966088 | tf_op jit(solution)/shard_map/ppermute | solution.py:17
  35.1 28.6 %collective-permute-start.1 = (bf16[2,1,80,2048]{3,2,1,0:T(8,128)(2,1)S(1)}, bf16[2,1,80,2048]{3,2,1,0:T(8,128)(2,1)S(1)}, u32[]{:S(2)}, u32[]{:S(2)}) collective-permute-start(bf16[2,1,80,2048]{3,2,1,0:T(8,128)(2,1)S(1)} %get-tuple-element.9), channel_id=1, source_target_pairs={{0,32},{32,0},{1,33},{33,1},{2,34},{34,2},{3,35},{35,3},{4,36},{36... | collective-permute-start | bytes 1966088 | tf_op jit(solution)/shard_map/ppermute | solution.py:17
  92.9 67.2 %all-to-all-start = ((bf16[2,2,80,2048]{3,1,0,2:T(2,128)(2,1)}), bf16[2,2,80,2048]{3,1,0,2:T(2,128)(2,1)S(1)}, u32[]{:S(2)}, u32[]{:S(2)}) async-start(bf16[2,2,80,2048]{3,1,0,2:T(2,128)(2,1)} %copy.104), calls=%async_computation | async-start | bytes 2621440 | tf_op jit(solution)/shard_map/all_to_all | solution.py:27
  99.1 182.6 %reduce-scatter.2.cloned.1.call-start = ((), (), s32[]{:S(2)}) async-start(), calls=%async_computation.6 | async-start | bytes 3538944 | tf_op jit(solution)/shard_map/reduce_scatter | solution.py:103
  100.2 4.0 %collective-permute-start.2 = (bf16[1,2,80,2048]{3,2,1,0:T(8,128)(2,1)S(1)}, bf16[1,2,80,2048]{3,2,1,0:T(8,128)(2,1)S(1)}, u32[]{:S(2)}, u32[]{:S(2)}) collective-permute-start(bf16[1,2,80,2048]{3,2,1,0:T(8,128)(2,1)S(1)} %copy.115), channel_id=1, source_target_pairs={{0,1},{1,0},{2,3},{3,2},{4,5},{5,4},{6,7},{7,6},{8,9},{9,8},{10,11... | collective-permute-start | bytes 1966088 | tf_op jit(solution)/shard_map/ppermute | solution.py:17
  105.4 56.4 %copy-start.1 = (bf16[2,1,80,2048]{3,2,1,0:T(8,128)(2,1)S(1)}, bf16[2,1,80,2048]{3,2,1,0:T(8,128)(2,1)}, u32[]{:S(2)}) copy-start(bf16[2,1,80,2048]{3,2,1,0:T(8,128)(2,1)} %get-tuple-element.4) | copy-start | bytes 1966084
  105.4 56.4 %collective-permute-start.3 = (bf16[2,1,80,2048]{3,2,1,0:T(8,128)(2,1)}, bf16[2,1,80,2048]{3,2,1,0:T(8,128)(2,1)}, u32[]{:S(2)}, u32[]{:S(2)}) collective-permute-start(bf16[2,1,80,2048]{3,2,1,0:T(8,128)(2,1)} %get-tuple-element.5), channel_id=1, source_target_pairs={{0,32},{32,0},{1,33},{33,1},{2,34},{34,2},{3,35},{35,3},{4,36},{36... | collective-permute-start | bytes 1966088 | tf_op jit(solution)/shard_map/ppermute | solution.py:17
  161.8 9.7 %copy-start.2 = (bf16[2,2,80,2048]{3,2,1,0:T(8,128)(2,1)S(1)}, bf16[2,2,80,2048]{3,2,1,0:T(8,128)(2,1)}, u32[]{:S(2)}) copy-start(bf16[2,2,80,2048]{3,2,1,0:T(8,128)(2,1)} %copy.105) | copy-start | bytes 3932164
  171.5 3.2 %copy-start.3 = (bf16[2,2,80,2048]{3,2,1,0:T(8,128)(2,1)S(1)}, bf16[2,2,80,2048]{3,2,1,0:T(8,128)(2,1)}, u32[]{:S(2)}) copy-start(bf16[2,2,80,2048]{3,2,1,0:T(8,128)(2,1)} %pad_maximum_fusion.1) | copy-start | bytes 3932164
  181.2 3.7 %copy-start.7 = (bf16[320,768]{1,0:T(8,128)(2,1)}, bf16[320,768]{1,0:T(8,128)(2,1)S(1)}, u32[]{:S(2)}) copy-start(bf16[320,768]{1,0:T(8,128)(2,1)S(1)} %get-tuple-element.3) | copy-start | bytes 1474564
  190.6 45.3 %all-to-all-start.2 = ((bf16[2,2,80,1024]{3,1,0,2:T(2,128)(2,1)}), bf16[2,2,80,1024]{3,1,0,2:T(2,128)(2,1)S(1)}, u32[]{:S(2)}, u32[]{:S(2)}) async-start(bf16[2,2,80,1024]{3,1,0,2:T(2,128)(2,1)} %copy.109), calls=%async_computation.2 | async-start | bytes 1310720 | tf_op jit(solution)/shard_map/all_to_all | solution.py:33
  207.4 14.7 %collective-permute-start.6 = (bf16[2,1,80,1024]{3,2,1,0:T(8,128)(2,1)S(1)}, bf16[2,1,80,1024]{3,2,1,0:T(8,128)(2,1)S(1)}, u32[]{:S(2)}, u32[]{:S(2)}) collective-permute-start(bf16[2,1,80,1024]{3,2,1,0:T(8,128)(2,1)S(1)} %get-tuple-element.19), channel_id=1, source_target_pairs={{0,32},{32,0},{1,33},{33,1},{2,34},{34,2},{3,35},{35,3},{4,36},{36... | collective-permute-start | bytes 983048 | tf_op jit(solution)/shard_map/ppermute | solution.py:17
  222.1 3.5 %collective-permute-start.7 = (bf16[1,2,80,1024]{3,2,1,0:T(8,128)(2,1)S(1)}, bf16[1,2,80,1024]{3,2,1,0:T(8,128)(2,1)S(1)}, u32[]{:S(2)}, u32[]{:S(2)}) collective-permute-start(bf16[1,2,80,1024]{3,2,1,0:T(8,128)(2,1)S(1)} %get-tuple-element.17), channel_id=1, source_target_pairs={{0,1},{1,0},{2,3},{3,2},{4,5},{5,4},{6,7},{7,6},{8,9},{9,8},{10,11... | collective-permute-start | bytes 983048 | tf_op jit(solution)/shard_map/ppermute | solution.py:17
  236.0 40.8 %all-to-all-start.3 = ((bf16[2,2,80,1024]{3,1,0,2:T(2,128)(2,1)}), bf16[2,2,80,1024]{3,1,0,2:T(2,128)(2,1)S(1)}, u32[]{:S(2)}, u32[]{:S(2)}) async-start(bf16[2,2,80,1024]{3,1,0,2:T(2,128)(2,1)} %copy.112), calls=%async_computation.3 | async-start | bytes 1310720 | tf_op jit(solution)/shard_map/all_to_all | solution.py:37
  244.6 10.9 %collective-permute-start.4 = (bf16[2,1,80,1024]{3,2,1,0:T(8,128)(2,1)S(1)}, bf16[2,1,80,1024]{3,2,1,0:T(8,128)(2,1)S(1)}, u32[]{:S(2)}, u32[]{:S(2)}) collective-permute-start(bf16[2,1,80,1024]{3,2,1,0:T(8,128)(2,1)S(1)} %copy.117), channel_id=1, source_target_pairs={{0,32},{32,0},{1,33},{33,1},{2,34},{34,2},{3,35},{35,3},{4,36},{36... | collective-permute-start | bytes 983048 | tf_op jit(solution)/shard_map/ppermute | solution.py:17
  255.6 21.4 %collective-permute-start.5 = (bf16[1,2,80,1024]{3,2,1,0:T(8,128)(2,1)S(1)}, bf16[1,2,80,1024]{3,2,1,0:T(8,128)(2,1)S(1)}, u32[]{:S(2)}, u32[]{:S(2)}) collective-permute-start(bf16[1,2,80,1024]{3,2,1,0:T(8,128)(2,1)S(1)} %get-tuple-element.13), channel_id=1, source_target_pairs={{0,1},{1,0},{2,3},{3,2},{4,5},{5,4},{6,7},{7,6},{8,9},{9,8},{10,11... | collective-permute-start | bytes 983048 | tf_op jit(solution)/shard_map/ppermute | solution.py:17
Sparse Core Ops, SparseCore 0:
  11.2 160.2 all-gather.1
  184.9 96.7 reduce-scatter.1

commit v3 on v2

--- a/solution.py
+++ b/solution.py
@@ -7,7 +7,8 @@
 TOP = 2
 CAP = 5
 SUB = ("ylo", "z", "core")
-ROWS = ("dp",) + SUB
+DP = ("x", "yhi")
+ROWS = DP + SUB
 SWAP = [(0, 1), (1, 0)]
 
 
@@ -38,6 +39,32 @@
     return x
 
 
+def gather_weights(w):
+    n_x = lax.axis_size("x")
+    n_y = lax.axis_size("yhi")
+    x_i = lax.axis_index("x")
+    y_i = lax.axis_index("yhi")
+    right = [(i, (i + 1) % n_x) for i in range(n_x)]
+    left = [(i, (i - 1) % n_x) for i in range(n_x)]
+    w_y = lax.ppermute(w, "yhi", SWAP)
+    from_left = lax.ppermute(w, "x", right)
+    from_right = lax.ppermute(w, "x", left)
+    y_from_left = lax.ppermute(w_y, "x", right)
+    y_from_right = lax.ppermute(w_y, "x", left)
+    far = lax.ppermute(from_right, "x", left)
+    y_far = lax.ppermute(y_from_left, "x", right)
+    pieces = [
+        (0, 0, w), (0, 1, w_y), (-1, 0, from_left), (1, 0, from_right),
+        (-1, 1, y_from_left), (1, 1, y_from_right), (2, 0, far), (2, 1, y_far),
+    ]
+    rows = w.shape[1]
+    full = jnp.zeros((w.shape[0], rows * n_x * n_y, w.shape[2]), w.dtype)
+    for dx, dy, piece in pieces:
+        owner = ((x_i + dx) % n_x) * n_y + (y_i ^ dy)
+        full = lax.dynamic_update_slice(full, piece, (0, owner * rows, 0))
+    return full
+
+
 def body(tokens, out_grad, combine, expert_ids, gate_weight, up_weight, down_weight):
     token_rows = tokens.shape[0]
     width = tokens.shape[1]
@@ -45,9 +72,7 @@
     expert_count = n_ylo * n_z * n_core
     capacity = CAP
     positions = expert_count * capacity
-    stacked = lax.all_gather(
-        jnp.concatenate([gate_weight, up_weight, down_weight], 0), "dp", axis=1, tiled=True
-    )
+    stacked = gather_weights(jnp.concatenate([gate_weight, up_weight, down_weight], 0))
     w_gate, w_up, w_down = stacked[0], stacked[1], stacked[2]
     flat_ids = expert_ids.reshape(-1)
     onehot = (flat_ids[:, None] == jnp.arange(expert_count, dtype=jnp.int32)[None, :]).astype(jnp.int32)
@@ -104,7 +129,7 @@
         lax.dot_general(
             grads_in, hidden, (((0,), (0,)), ((), ())), preferred_element_type=jnp.float32
         ).astype(jnp.bfloat16),
-        "dp",
+        DP,
         scatter_dimension=0,
         tiled=True,
     )
@@ -113,9 +138,9 @@
 
 def solution(mesh):
     n_dp, n_expert = mesh.devices.shape
-    fine = Mesh(mesh.devices.reshape(n_dp, 2, n_expert // 4, 2), ("dp",) + SUB)
+    fine = Mesh(mesh.devices.reshape(n_dp // 2, 2, 2, n_expert // 4, 2), DP + SUB)
     rows = P(ROWS, None)
-    weights = P(SUB, "dp", None)
+    weights = P(SUB, DP, None)
     return jax.shard_map(
         body,
         mesh=fine,

time: 289 us -> 301 us (1.042)
  starting transfers between devices: 61.4 us -> 85.8 us
  waiting for transfers between devices: 167 us -> 147 us
  local copies, waits for them, and re-layouts: 15.2 us -> 26.7 us
  other arithmetic: 7.24 us -> 3.19 us
    ppermute x0 -> x7, waiting for transfers between devices: none -> 53.5 us  [the longest x1 22.6 us: gather_weights(): y_from_left = lax.ppermute(w_y, 'x', right)]
    all_to_all x2, waiting for transfers between devices: 77.3 us -> 35.5 us  [forward_move(): x = lax.all_to_all(x, 'z', 2, 2, tiled=True)]
    ppermute x8, waiting for transfers between devices: 50.9 us -> 22.4 us  [swap_half(): got = lax.ppermute(go, axis_name, SWAP)]
    ppermute x0 -> x7, starting transfers between devices: none -> 22.8 us  [the longest x1 4.8 us: gather_weights(): w_y = lax.ppermute(w, 'yhi', SWAP)]
    all_gather x1 -> x0, waiting for transfers between devices: 7.29 us -> none  [body(): lax.all_gather(jnp.concatenate([gate_weight, up_weight, down_weight], 0),...]
    dynamic_update_slice x0 -> x8, local copies, waits for them, and re-layouts: none -> 7.25 us  [gather_weights(): full = lax.dynamic_update_slice(full, piece, (0, owner * rows, 0))]
    unnamed x22 -> x30, local copies, waits for them, and re-layouts: 1.04 us -> 5.96 us
  transfers between devices with their start and end apart: 14 -> 20, of which waited for: 12 -> 12; matrix products, arithmetic and copies ran while one was open for 10% -> 12% of each run, Pallas kernels for 0% -> 0%
where the time goes in v3:
time: 301 us; the launch traced here: 300 us
  waiting for transfers between devices  147 us (49%)
  starting transfers between devices  85.8 us (29%)
  local copies, waits for them, and re-layouts  26.7 us (9%)
  matrix products  22.4 us (7%)
  between operations  14.7 us (5%)
  other arithmetic  3.19 us (1%)
    all_to_all x2, waiting for transfers between devices, forward_move(): x = lax.all_to_all(x, 'z', 2, 2, tiled=True)  35.5 us
    all_to_all x2, waiting for transfers between devices, backward_move(): x = lax.all_to_all(x, 'z', 2, 2, tiled=True)  30.9 us
    ppermute x1, waiting for transfers between devices, gather_weights(): y_from_left = lax.ppermute(w_y, 'x', right)  22.6 us
    ppermute x8, waiting for transfers between devices, swap_half(): got = lax.ppermute(go, axis_name, SWAP)  22.4 us
    ppermute x8, starting transfers between devices, swap_half(): got = lax.ppermute(go, axis_name, SWAP)  21.9 us
    all_to_all x2, starting transfers between devices, forward_move(): x = lax.all_to_all(x, 'z', 2, 2, tiled=True)  21.5 us
    all_to_all x2, starting transfers between devices, backward_move(): x = lax.all_to_all(x, 'z', 2, 2, tiled=True)  19.5 us
    ppermute x1, waiting for transfers between devices, gather_weights(): y_far = lax.ppermute(y_from_left, 'x', right)  18.1 us
  transfers between devices with their start and end apart: 20, of which 12 were waited for; matrix products, arithmetic and copies ran while one was open for 12% of the time, Pallas kernels for 0%

profile of v3, /device:TPU:6, one launch (start us, length us, event | category | flops | bytes accessed | tf_op | source)
XLA Modules:
  0.0 300.2 jit_solution(2510379013332192663)
XLA Ops:
  7.2 0.8 copy.91
  8.3 0.7 broadcast_compare_fusion
  9.0 0.6 reduce-window.6
  10.5 0.5 convolution_convert_fusion.1
  11.0 2.4 copy.106
  13.5 15.3 %all-to-all-start.1 = ((bf16[2,2,80,2048]{3,1,0,2:T(2,128)(2,1)}), bf16[2,2,80,2048]{3,1,0,2:T(2,128)(2,1)S(1)}, u32[]{:S(2)}, u32[]{:S(2)}) async-start(bf16[2,2,80,2048]{3,1,0,2:T(2,128)(2,1)} %copy.106), calls=%async_computation.1 | async-start | bytes 2621440 | tf_op jit(solution)/shard_map/all_to_all | solution.py:24
  29.2 0.5 fusion.3
  29.9 1.9 collective-permute-start
  31.8 2.1 collective-permute-done
  34.0 3.6 %collective-permute-start.1 = (bf16[2,1,80,2048]{3,2,1,0:T(8,128)(2,1)S(1)}, bf16[2,1,80,2048]{3,2,1,0:T(8,128)(2,1)S(1)}, u32[]{:S(2)}, u32[]{:S(2)}) collective-permute-start(bf16[2,1,80,2048]{3,2,1,0:T(8,128)(2,1)S(1)} %get-tuple-element.9), channel_id=1, source_target_pairs={{0,32},{32,0},{1,33},{33,1},{2,34},{34,2},{3,35},{35,3},{4,36},{36... | collective-permute-start | bytes 1966088 | tf_op jit(solution)/shard_map/ppermute | solution.py:18
  37.7 0.8 constant_dynamic-update-slice_fusion.2
  38.4 0.8 constant_dynamic-update-slice_fusion.1
  39.2 0.8 constant_dynamic-update-slice_fusion
  40.0 4.8 %collective-permute-start.2 = (bf16[3,256,768]{2,1,0:T(8,128)(2,1)}, bf16[3,256,768]{2,1,0:T(8,128)(2,1)}, u32[]{:S(2)}, u32[]{:S(2)}) collective-permute-start(bf16[3,256,768]{2,1,0:T(8,128)(2,1)} %constant_dynamic-update-slice_fusion), channel_id=1, source_target_pairs={{0,64},{64,0},{1,65},{65,1},{2,66},{66,2},{3,67},{67,3},{4,68},{68... | collective-permute-start | bytes 3538952 | tf_op jit(solution)/shard_map/ppermute | solution.py:49
  44.8 2.7 collective-permute-start.4
  47.5 6.1 %collective-permute-done.1 = bf16[2,1,80,2048]{3,2,1,0:T(8,128)(2,1)S(1)} collective-permute-done((bf16[2,1,80,2048]{3,2,1,0:T(8,128)(2,1)S(1)}, bf16[2,1,80,2048]{3,2,1,0:T(8,128)(2,1)S(1)}, u32[]{:S(2)}, u32[]{:S(2)}) %collective-permute-start.1) | collective-permute-done | bytes 655392 | tf_op jit(solution)/shard_map/ppermute | solution.py:18
  53.7 2.4 copy.104
  56.2 35.5 %all-to-all-done.1 = bf16[2,2,80,2048]{3,1,0,2:T(2,128)(2,1)S(1)} async-done(((bf16[2,2,80,2048]{3,1,0,2:T(2,128)(2,1)}), bf16[2,2,80,2048]{3,1,0,2:T(2,128)(2,1)S(1)}, u32[]{:S(2)}, u32[]{:S(2)}) %all-to-all-start.1) | async-done | bytes 1310752 | tf_op jit(solution)/shard_map/all_to_all | solution.py:24
  91.7 6.2 %all-to-all-start = ((bf16[2,2,80,2048]{3,1,0,2:T(2,128)(2,1)}), bf16[2,2,80,2048]{3,1,0,2:T(2,128)(2,1)S(1)}, u32[]{:S(2)}, u32[]{:S(2)}) async-start(bf16[2,2,80,2048]{3,1,0,2:T(2,128)(2,1)} %copy.104), calls=%async_computation | async-start | bytes 2621440 | tf_op jit(solution)/shard_map/all_to_all | solution.py:28
  97.9 2.4 collective-permute-start.3
  100.4 3.4 %collective-permute-start.5 = (bf16[3,256,768]{2,1,0:T(8,128)(2,1)}, bf16[3,256,768]{2,1,0:T(8,128)(2,1)}, u32[]{:S(2)}, u32[]{:S(2)}) collective-permute-start(bf16[3,256,768]{2,1,0:T(8,128)(2,1)} %collective-permute-done.2), channel_id=1, source_target_pairs={{0,128},{128,256},{256,384},{384,0},{1,129},{129,257},{257,385},{3... | collective-permute-start | bytes 3538952 | tf_op jit(solution)/shard_map/ppermute | solution.py:52
  103.9 0.6 broadcast_in_dim.27
  104.5 1.4 constant_dynamic-update-slice_fusion.12
  105.9 2.4 collective-permute-start.6
  108.3 3.5 %collective-permute-start.7 = (bf16[3,256,768]{2,1,0:T(8,128)(2,1)}, bf16[3,256,768]{2,1,0:T(8,128)(2,1)S(1)}, u32[]{:S(2)}, u32[]{:S(2)}) collective-permute-start(bf16[3,256,768]{2,1,0:T(8,128)(2,1)} %collective-permute-done.4), channel_id=1, source_target_pairs={{0,384},{128,0},{256,128},{384,256},{1,385},{129,1},{257,129},{385... | collective-permute-start | bytes 3538952 | tf_op jit(solution)/shard_map/ppermute | solution.py:54
  111.8 0.9 fusion.39
  112.9 1.9 collective-permute-start.9
  114.8 1.4 constant_dynamic-update-slice_fusion.11
  116.2 12.8 %collective-permute-done.3 = bf16[3,256,768]{2,1,0:T(8,128)(2,1)} collective-permute-done((bf16[3,256,768]{2,1,0:T(8,128)(2,1)}, bf16[3,256,768]{2,1,0:T(8,128)(2,1)}, u32[]{:S(2)}, u32[]{:S(2)}) %collective-permute-start.3) | collective-permute-done | bytes 1179680 | tf_op jit(solution)/shard_map/ppermute | solution.py:50
  129.0 1.4 constant_dynamic-update-slice_fusion.10
  130.4 22.6 %collective-permute-done.5 = bf16[3,256,768]{2,1,0:T(8,128)(2,1)} collective-permute-done((bf16[3,256,768]{2,1,0:T(8,128)(2,1)}, bf16[3,256,768]{2,1,0:T(8,128)(2,1)}, u32[]{:S(2)}, u32[]{:S(2)}) %collective-permute-start.5) | collective-permute-done | bytes 1179680 | tf_op jit(solution)/shard_map/ppermute | solution.py:52
  153.0 3.6 %collective-permute-start.8 = (bf16[3,256,768]{2,1,0:T(8,128)(2,1)}, bf16[3,256,768]{2,1,0:T(8,128)(2,1)S(1)}, u32[]{:S(2)}, u32[]{:S(2)}) collective-permute-start(bf16[3,256,768]{2,1,0:T(8,128)(2,1)} %collective-permute-done.5), channel_id=1, source_target_pairs={{0,128},{128,256},{256,384},{384,0},{1,129},{129,257},{257,385},{3... | collective-permute-start | bytes 3538952 | tf_op jit(solution)/shard_map/ppermute | solution.py:55
  157.1 3.7 %collective-permute-start.10 = (bf16[2,1,80,2048]{3,2,1,0:T(8,128)(2,1)S(1)}, bf16[2,1,80,2048]{3,2,1,0:T(8,128)(2,1)S(1)}, u32[]{:S(2)}, u32[]{:S(2)}) collective-permute-start(bf16[2,1,80,2048]{3,2,1,0:T(8,128)(2,1)S(1)} %get-tuple-element.5), channel_id=1, source_target_pairs={{0,32},{32,0},{1,33},{33,1},{2,34},{34,2},{3,35},{35,3},{4,36},{36... | collective-permute-start | bytes 1966088 | tf_op jit(solution)/shard_map/ppermute | solution.py:18
  160.7 1.4 constant_dynamic-update-slice_fusion.9
  162.1 1.4 constant_dynamic-update-slice_fusion.8
  163.8 18.1 %collective-permute-done.8 = bf16[3,256,768]{2,1,0:T(8,128)(2,1)S(1)} collective-permute-done((bf16[3,256,768]{2,1,0:T(8,128)(2,1)}, bf16[3,256,768]{2,1,0:T(8,128)(2,1)S(1)}, u32[]{:S(2)}, u32[]{:S(2)}) %collective-permute-start.8) | collective-permute-done | bytes 1179680 | tf_op jit(solution)/shard_map/ppermute | solution.py:55
  182.1 2.7 fusion.1
  184.9 1.1 copy-done.1
  185.9 2.2 fusion
  188.2 0.7 copy.105
  188.9 0.5 copy-done.9
  189.7 3.6 %convolution_convert_fusion = bf16[2048,768]{1,0:T(8,128)(2,1)} fusion(bf16[320,2048]{1,0:T(8,128)(2,1)S(1)} %bitcast.82, f32[320,768]{1,0:T(8,128)S(1)} %copy-done.9, f32[320,768]{1,0:T(8,128)S(1)} %copy-done.10), kind=kOutput, calls=%fused_computation | convolution fusion | flops 1009680384 | bytes 6422528 | tf_op jit(solution)/shard_map/dot_general | solution.py:129
  193.3 3.8 %multiply_convert_fusion.2 = (bf16[320,768]{1,0:T(8,128)(2,1)S(1)}, bf16[320,768]{1,0:T(8,128)(2,1)S(1)}) fusion(f32[320,768]{1,0:T(8,128)} %fusion, f32[320,768]{1,0:T(8,128)} %fusion.1, bf16[320,2048]{1,0:T(8,128)(2,1)S(1)} %bitcast.83, bf16[3,2048,768]{2,1,0:T(8,128)(2,1)} %copy-done.1), kind=kOutput, calls=%fused_computation.30 | convolution fusion | flops 1009827840 | bytes 7405568 | tf_op jit(solution)/shard_map/dot_general | solution.py:104
  197.1 0.7 copy-done.7
  197.8 2.1 fusion.6
  200.0 2.1 fusion.11
  202.1 1.6 copy.109
  203.7 11.4 %all-to-all-start.2 = ((bf16[2,2,80,1024]{3,1,0,2:T(2,128)(2,1)}), bf16[2,2,80,1024]{3,1,0,2:T(2,128)(2,1)S(1)}, u32[]{:S(2)}, u32[]{:S(2)}) async-start(bf16[2,2,80,1024]{3,1,0,2:T(2,128)(2,1)} %copy.109), calls=%async_computation.2 | async-start | bytes 1310720 | tf_op jit(solution)/shard_map/all_to_all | solution.py:34
  215.1 2.1 fusion.4
  217.3 2.1 fusion.10
  219.4 3.5 %collective-permute-start.13 = (bf16[2,1,80,1024]{3,2,1,0:T(8,128)(2,1)S(1)}, bf16[2,1,80,1024]{3,2,1,0:T(8,128)(2,1)S(1)}, u32[]{:S(2)}, u32[]{:S(2)}) collective-permute-start(bf16[2,1,80,1024]{3,2,1,0:T(8,128)(2,1)S(1)} %get-tuple-element.19), channel_id=1, source_target_pairs={{0,32},{32,0},{1,33},{33,1},{2,34},{34,2},{3,35},{35,3},{4,36},{36... | collective-permute-start | bytes 983048 | tf_op jit(solution)/shard_map/ppermute | solution.py:18
  222.9 6.1 %collective-permute-done.13 = bf16[2,1,80,1024]{3,2,1,0:T(8,128)(2,1)S(1)} collective-permute-done((bf16[2,1,80,1024]{3,2,1,0:T(8,128)(2,1)S(1)}, bf16[2,1,80,1024]{3,2,1,0:T(8,128)(2,1)S(1)}, u32[]{:S(2)}, u32[]{:S(2)}) %collective-permute-start.13) | collective-permute-done | bytes 327712 | tf_op jit(solution)/shard_map/ppermute | solution.py:18
  229.1 1.9 collective-permute-start.14
  231.0 1.6 collective-permute-done.14
  232.7 1.5 copy.112
  234.2 11.7 %all-to-all-done.2 = bf16[2,2,80,1024]{3,1,0,2:T(2,128)(2,1)S(1)} async-done(((bf16[2,2,80,1024]{3,1,0,2:T(2,128)(2,1)}), bf16[2,2,80,1024]{3,1,0,2:T(2,128)(2,1)S(1)}, u32[]{:S(2)}, u32[]{:S(2)}) %all-to-all-start.2) | async-done | bytes 655392 | tf_op jit(solution)/shard_map/all_to_all | solution.py:34
  245.9 8.0 %all-to-all-start.3 = ((bf16[2,2,80,1024]{3,1,0,2:T(2,128)(2,1)}), bf16[2,2,80,1024]{3,1,0,2:T(2,128)(2,1)S(1)}, u32[]{:S(2)}, u32[]{:S(2)}) async-start(bf16[2,2,80,1024]{3,1,0,2:T(2,128)(2,1)} %copy.112), calls=%async_computation.3 | async-start | bytes 1310720 | tf_op jit(solution)/shard_map/all_to_all | solution.py:38
  253.9 0.9 fusion.42
  255.0 3.5 %collective-permute-start.11 = (bf16[2,1,80,1024]{3,2,1,0:T(8,128)(2,1)S(1)}, bf16[2,1,80,1024]{3,2,1,0:T(8,128)(2,1)S(1)}, u32[]{:S(2)}, u32[]{:S(2)}) collective-permute-start(bf16[2,1,80,1024]{3,2,1,0:T(8,128)(2,1)S(1)} %copy.117), channel_id=1, source_target_pairs={{0,32},{32,0},{1,33},{33,1},{2,34},{34,2},{3,35},{35,3},{4,36},{36... | collective-permute-start | bytes 983048 | tf_op jit(solution)/shard_map/ppermute | solution.py:18
  258.7 6.5 %collective-permute-done.11 = bf16[2,1,80,1024]{3,2,1,0:T(8,128)(2,1)S(1)} collective-permute-done((bf16[2,1,80,1024]{3,2,1,0:T(8,128)(2,1)S(1)}, bf16[2,1,80,1024]{3,2,1,0:T(8,128)(2,1)S(1)}, u32[]{:S(2)}, u32[]{:S(2)}) %collective-permute-start.11) | collective-permute-done | bytes 327712 | tf_op jit(solution)/shard_map/ppermute | solution.py:18
  265.3 1.9 collective-permute-start.12
  267.3 19.3 %all-to-all-done.3 = bf16[2,2,80,1024]{3,1,0,2:T(2,128)(2,1)S(1)} async-done(((bf16[2,2,80,1024]{3,1,0,2:T(2,128)(2,1)}), bf16[2,2,80,1024]{3,1,0,2:T(2,128)(2,1)S(1)}, u32[]{:S(2)}, u32[]{:S(2)}) %all-to-all-start.3) | async-done | bytes 655392 | tf_op jit(solution)/shard_map/all_to_all | solution.py:38
  287.4 0.8 pad_maximum_fusion.5
  288.3 5.1 %reduce-scatter.2.cloned.1.call-done = bf16[256,768]{1,0:T(8,128)(2,1)} async-done(((bf16[2048,768]{1,0:T(8,128)(2,1)}), bf16[256,768]{1,0:T(8,128)(2,1)}) %reduce-scatter.2.cloned.1.call-update) | async-done | bytes 393232 | tf_op jit(solution)/shard_map/reduce_scatter | solution.py:128
  (67 shorter events, 4.9 us)
Async XLA Ops:
  7.2 3.4 %copy-start = (bf16[128,2048]{1,0:T(8,128)(2,1)S(1)}, bf16[128,2048]{1,0:T(8,128)(2,1)}, u32[]{:S(2)}) copy-start(bf16[128,2048]{1,0:T(8,128)(2,1)} %param.7) | copy-start | bytes 1572868
  13.5 15.3 %copy-start.6 = (f32[128,2]{0,1:T(2,128)S(1)}, f32[128,2]{0,1:T(2,128)}, u32[]{:S(2)}) copy-start(f32[128,2]{0,1:T(2,128)} %param.9) | copy-start | bytes 3076
  13.5 15.8 %copy-start.2 = (bf16[128,2048]{1,0:T(8,128)(2,1)S(1)}, bf16[128,2048]{1,0:T(8,128)(2,1)}, u32[]{:S(2)}) copy-start(bf16[128,2048]{1,0:T(8,128)(2,1)} %param.8) | copy-start | bytes 1572868
  13.5 78.2 %all-to-all-start.1 = ((bf16[2,2,80,2048]{3,1,0,2:T(2,128)(2,1)}), bf16[2,2,80,2048]{3,1,0,2:T(2,128)(2,1)S(1)}, u32[]{:S(2)}, u32[]{:S(2)}) async-start(bf16[2,2,80,2048]{3,1,0,2:T(2,128)(2,1)} %copy.106), calls=%async_computation.1 | async-start | bytes 2621440 | tf_op jit(solution)/shard_map/all_to_all | solution.py:24
  29.9 4.0 %collective-permute-start = (bf16[1,2,80,2048]{3,2,1,0:T(8,128)(2,1)S(1)}, bf16[1,2,80,2048]{3,2,1,0:T(8,128)(2,1)S(1)}, u32[]{:S(2)}, u32[]{:S(2)}) collective-permute-start(bf16[1,2,80,2048]{3,2,1,0:T(8,128)(2,1)S(1)} %bitcast.86), channel_id=1, source_target_pairs={{0,1},{1,0},{2,3},{3,2},{4,5},{5,4},{6,7},{7,6},{8,9},{9,8},{10,11... | collective-permute-start | bytes 1966088 | tf_op jit(solution)/shard_map/ppermute | solution.py:18
  33.9 3.8 %copy-start.3 = (bf16[1,256,768]{2,1,0:T(8,128)(2,1)S(1)}, bf16[1,256,768]{2,1,0:T(8,128)(2,1)}, u32[]{:S(2)}) copy-start(bf16[1,256,768]{2,1,0:T(8,128)(2,1)} %param.11) | copy-start | bytes 1179652
  33.9 4.6 %copy-start.4 = (bf16[1,256,768]{2,1,0:T(8,128)(2,1)S(1)}, bf16[1,256,768]{2,1,0:T(8,128)(2,1)}, u32[]{:S(2)}) copy-start(bf16[1,256,768]{2,1,0:T(8,128)(2,1)} %param.12) | copy-start | bytes 1179652
  34.0 5.2 %copy-start.5 = (bf16[1,256,768]{2,1,0:T(8,128)(2,1)S(1)}, bf16[1,256,768]{2,1,0:T(8,128)(2,1)}, u32[]{:S(2)}) copy-start(bf16[1,256,768]{2,1,0:T(8,128)(2,1)} %param.13) | copy-start | bytes 1179652
  34.0 19.6 %collective-permute-start.1 = (bf16[2,1,80,2048]{3,2,1,0:T(8,128)(2,1)S(1)}, bf16[2,1,80,2048]{3,2,1,0:T(8,128)(2,1)S(1)}, u32[]{:S(2)}, u32[]{:S(2)}) collective-permute-start(bf16[2,1,80,2048]{3,2,1,0:T(8,128)(2,1)S(1)} %get-tuple-element.9), channel_id=1, source_target_pairs={{0,32},{32,0},{1,33},{33,1},{2,34},{34,2},{3,35},{35,3},{4,36},{36... | collective-permute-start | bytes 1966088 | tf_op jit(solution)/shard_map/ppermute | solution.py:18
  40.0 60.3 %collective-permute-start.2 = (bf16[3,256,768]{2,1,0:T(8,128)(2,1)}, bf16[3,256,768]{2,1,0:T(8,128)(2,1)}, u32[]{:S(2)}, u32[]{:S(2)}) collective-permute-start(bf16[3,256,768]{2,1,0:T(8,128)(2,1)} %constant_dynamic-update-slice_fusion), channel_id=1, source_target_pairs={{0,64},{64,0},{1,65},{65,1},{2,66},{66,2},{3,67},{67,3},{4,68},{68... | collective-permute-start | bytes 3538952 | tf_op jit(solution)/shard_map/ppermute | solution.py:49
  44.8 63.5 %collective-permute-start.4 = (bf16[3,256,768]{2,1,0:T(8,128)(2,1)}, bf16[3,256,768]{2,1,0:T(8,128)(2,1)}, u32[]{:S(2)}, u32[]{:S(2)}) collective-permute-start(bf16[3,256,768]{2,1,0:T(8,128)(2,1)} %constant_dynamic-update-slice_fusion), channel_id=1, source_target_pairs={{0,384},{128,0},{256,128},{384,256},{1,385},{129,1},{257,129},{385... | collective-permute-start | bytes 3538952 | tf_op jit(solution)/shard_map/ppermute | solution.py:51
  91.7 96.5 %all-to-all-start = ((bf16[2,2,80,2048]{3,1,0,2:T(2,128)(2,1)}), bf16[2,2,80,2048]{3,1,0,2:T(2,128)(2,1)S(1)}, u32[]{:S(2)}, u32[]{:S(2)}) async-start(bf16[2,2,80,2048]{3,1,0,2:T(2,128)(2,1)} %copy.104), calls=%async_computation | async-start | bytes 2621440 | tf_op jit(solution)/shard_map/all_to_all | solution.py:28
  97.9 195.4 %reduce-scatter.2.cloned.1.call-start = ((), (), s32[]{:S(2)}) async-start(), calls=%async_computation.5 | async-start | bytes 3538944 | tf_op jit(solution)/shard_map/reduce_scatter | solution.py:128
  97.9 31.1 %collective-permute-start.3 = (bf16[3,256,768]{2,1,0:T(8,128)(2,1)}, bf16[3,256,768]{2,1,0:T(8,128)(2,1)}, u32[]{:S(2)}, u32[]{:S(2)}) collective-permute-start(bf16[3,256,768]{2,1,0:T(8,128)(2,1)} %constant_dynamic-update-slice_fusion), channel_id=1, source_target_pairs={{0,128},{128,256},{256,384},{384,0},{1,129},{129,257},{257,385},{3... | collective-permute-start | bytes 3538952 | tf_op jit(solution)/shard_map/ppermute | solution.py:50
  100.4 52.7 %collective-permute-start.5 = (bf16[3,256,768]{2,1,0:T(8,128)(2,1)}, bf16[3,256,768]{2,1,0:T(8,128)(2,1)}, u32[]{:S(2)}, u32[]{:S(2)}) collective-permute-start(bf16[3,256,768]{2,1,0:T(8,128)(2,1)} %collective-permute-done.2), channel_id=1, source_target_pairs={{0,128},{128,256},{256,384},{384,0},{1,129},{129,257},{257,385},{3... | collective-permute-start | bytes 3538952 | tf_op jit(solution)/shard_map/ppermute | solution.py:52
  105.9 57.7 %collective-permute-start.6 = (bf16[3,256,768]{2,1,0:T(8,128)(2,1)}, bf16[3,256,768]{2,1,0:T(8,128)(2,1)S(1)}, u32[]{:S(2)}, u32[]{:S(2)}) collective-permute-start(bf16[3,256,768]{2,1,0:T(8,128)(2,1)} %collective-permute-done.2), channel_id=1, source_target_pairs={{0,384},{128,0},{256,128},{384,256},{1,385},{129,1},{257,129},{385... | collective-permute-start | bytes 3538952 | tf_op jit(solution)/shard_map/ppermute | solution.py:53
  108.3 55.3 %collective-permute-start.7 = (bf16[3,256,768]{2,1,0:T(8,128)(2,1)}, bf16[3,256,768]{2,1,0:T(8,128)(2,1)S(1)}, u32[]{:S(2)}, u32[]{:S(2)}) collective-permute-start(bf16[3,256,768]{2,1,0:T(8,128)(2,1)} %collective-permute-done.4), channel_id=1, source_target_pairs={{0,384},{128,0},{256,128},{384,256},{1,385},{129,1},{257,129},{385... | collective-permute-start | bytes 3538952 | tf_op jit(solution)/shard_map/ppermute | solution.py:54
  112.9 43.9 %collective-permute-start.9 = (bf16[1,2,80,2048]{3,2,1,0:T(8,128)(2,1)S(1)}, bf16[1,2,80,2048]{3,2,1,0:T(8,128)(2,1)S(1)}, u32[]{:S(2)}, u32[]{:S(2)}) collective-permute-start(bf16[1,2,80,2048]{3,2,1,0:T(8,128)(2,1)S(1)} %copy.115), channel_id=1, source_target_pairs={{0,1},{1,0},{2,3},{3,2},{4,5},{5,4},{6,7},{7,6},{8,9},{9,8},{10,11... | collective-permute-start | bytes 1966088 | tf_op jit(solution)/shard_map/ppermute | solution.py:18
  153.0 28.8 %collective-permute-start.8 = (bf16[3,256,768]{2,1,0:T(8,128)(2,1)}, bf16[3,256,768]{2,1,0:T(8,128)(2,1)S(1)}, u32[]{:S(2)}, u32[]{:S(2)}) collective-permute-start(bf16[3,256,768]{2,1,0:T(8,128)(2,1)} %collective-permute-done.5), channel_id=1, source_target_pairs={{0,128},{128,256},{256,384},{384,0},{1,129},{129,257},{257,385},{3... | collective-permute-start | bytes 3538952 | tf_op jit(solution)/shard_map/ppermute | solution.py:55
  157.1 24.9 %collective-permute-start.10 = (bf16[2,1,80,2048]{3,2,1,0:T(8,128)(2,1)S(1)}, bf16[2,1,80,2048]{3,2,1,0:T(8,128)(2,1)S(1)}, u32[]{:S(2)}, u32[]{:S(2)}) collective-permute-start(bf16[2,1,80,2048]{3,2,1,0:T(8,128)(2,1)S(1)} %get-tuple-element.5), channel_id=1, source_target_pairs={{0,32},{32,0},{1,33},{33,1},{2,34},{34,2},{3,35},{35,3},{4,36},{36... | collective-permute-start | bytes 1966088 | tf_op jit(solution)/shard_map/ppermute | solution.py:18
  182.0 4.0 %copy-start.1 = (bf16[3,2048,768]{2,1,0:T(8,128)(2,1)}, bf16[3,2048,768]{2,1,0:T(8,128)(2,1)S(1)}, u32[]{:S(2)}) copy-start(bf16[3,2048,768]{2,1,0:T(8,128)(2,1)S(1)} %constant_dynamic-update-slice_fusion.5) | copy-start | bytes 28311556
  188.2 1.2 copy-start.9
  188.2 1.5 copy-start.10
  197.1 0.8 copy-start.7
  202.1 13.0 %copy-start.8 = (bf16[320,768]{1,0:T(8,128)(2,1)S(1)}, bf16[320,768]{1,0:T(8,128)(2,1)}, u32[]{:S(2)}) copy-start(bf16[320,768]{1,0:T(8,128)(2,1)} %copy-done.7) | copy-start | bytes 1474564
  203.7 42.2 %all-to-all-start.2 = ((bf16[2,2,80,1024]{3,1,0,2:T(2,128)(2,1)}), bf16[2,2,80,1024]{3,1,0,2:T(2,128)(2,1)S(1)}, u32[]{:S(2)}, u32[]{:S(2)}) async-start(bf16[2,2,80,1024]{3,1,0,2:T(2,128)(2,1)} %copy.109), calls=%async_computation.2 | async-start | bytes 1310720 | tf_op jit(solution)/shard_map/all_to_all | solution.py:34
  219.4 9.6 %collective-permute-start.13 = (bf16[2,1,80,1024]{3,2,1,0:T(8,128)(2,1)S(1)}, bf16[2,1,80,1024]{3,2,1,0:T(8,128)(2,1)S(1)}, u32[]{:S(2)}, u32[]{:S(2)}) collective-permute-start(bf16[2,1,80,1024]{3,2,1,0:T(8,128)(2,1)S(1)} %get-tuple-element.19), channel_id=1, source_target_pairs={{0,32},{32,0},{1,33},{33,1},{2,34},{34,2},{3,35},{35,3},{4,36},{36... | collective-permute-start | bytes 983048 | tf_op jit(solution)/shard_map/ppermute | solution.py:18
  229.1 3.5 %collective-permute-start.14 = (bf16[1,2,80,1024]{3,2,1,0:T(8,128)(2,1)S(1)}, bf16[1,2,80,1024]{3,2,1,0:T(8,128)(2,1)S(1)}, u32[]{:S(2)}, u32[]{:S(2)}) collective-permute-start(bf16[1,2,80,1024]{3,2,1,0:T(8,128)(2,1)S(1)} %get-tuple-element.17), channel_id=1, source_target_pairs={{0,1},{1,0},{2,3},{3,2},{4,5},{5,4},{6,7},{7,6},{8,9},{9,8},{10,11... | collective-permute-start | bytes 983048 | tf_op jit(solution)/shard_map/ppermute | solution.py:18
  245.9 40.6 %all-to-all-start.3 = ((bf16[2,2,80,1024]{3,1,0,2:T(2,128)(2,1)}), bf16[2,2,80,1024]{3,1,0,2:T(2,128)(2,1)S(1)}, u32[]{:S(2)}, u32[]{:S(2)}) async-start(bf16[2,2,80,1024]{3,1,0,2:T(2,128)(2,1)} %copy.112), calls=%async_computation.3 | async-start | bytes 1310720 | tf_op jit(solution)/shard_map/all_to_all | solution.py:38
  255.0 10.2 %collective-permute-start.11 = (bf16[2,1,80,1024]{3,2,1,0:T(8,128)(2,1)S(1)}, bf16[2,1,80,1024]{3,2,1,0:T(8,128)(2,1)S(1)}, u32[]{:S(2)}, u32[]{:S(2)}) collective-permute-start(bf16[2,1,80,1024]{3,2,1,0:T(8,128)(2,1)S(1)} %copy.117), channel_id=1, source_target_pairs={{0,32},{32,0},{1,33},{33,1},{2,34},{34,2},{3,35},{35,3},{4,36},{36... | collective-permute-start | bytes 983048 | tf_op jit(solution)/shard_map/ppermute | solution.py:18
  265.3 21.4 %collective-permute-start.12 = (bf16[1,2,80,1024]{3,2,1,0:T(8,128)(2,1)S(1)}, bf16[1,2,80,1024]{3,2,1,0:T(8,128)(2,1)S(1)}, u32[]{:S(2)}, u32[]{:S(2)}) collective-permute-start(bf16[1,2,80,1024]{3,2,1,0:T(8,128)(2,1)S(1)} %get-tuple-element.13), channel_id=1, source_target_pairs={{0,1},{1,0},{2,3},{3,2},{4,5},{5,4},{6,7},{7,6},{8,9},{9,8},{10,11... | collective-permute-start | bytes 983048 | tf_op jit(solution)/shard_map/ppermute | solution.py:18
Sparse Core Ops, SparseCore 0:
  197.2 96.0 reduce-scatter.1

commit v4 on v3

--- a/solution.py
+++ b/solution.py
@@ -72,8 +72,9 @@
     expert_count = n_ylo * n_z * n_core
     capacity = CAP
     positions = expert_count * capacity
-    stacked = gather_weights(jnp.concatenate([gate_weight, up_weight, down_weight], 0))
-    w_gate, w_up, w_down = stacked[0], stacked[1], stacked[2]
+    stacked = lax.all_gather(jnp.concatenate([gate_weight, up_weight], 0), DP, axis=1, tiled=True)
+    w_gate, w_up = stacked[0], stacked[1]
+    w_down = gather_weights(down_weight)[0]
     flat_ids = expert_ids.reshape(-1)
     onehot = (flat_ids[:, None] == jnp.arange(expert_count, dtype=jnp.int32)[None, :]).astype(jnp.int32)
     earlier = jnp.cumsum(onehot, axis=0) - onehot

time: 301 us -> 284 us (0.944)
  waiting for transfers between devices: 147 us -> 127 us
    ppermute x8, waiting for transfers between devices: 22.4 us -> 52.8 us  [swap_half(): got = lax.ppermute(go, axis_name, SWAP)]
    ppermute x1, waiting for transfers between devices: 22.6 us -> 4.54 us  [gather_weights(): y_from_left = lax.ppermute(w_y, 'x', right)]
    ppermute x1, waiting for transfers between devices: 18.1 us -> 0.01 us  [gather_weights(): y_far = lax.ppermute(y_from_left, 'x', right)]
    ppermute x1, waiting for transfers between devices: 12.8 us -> 0.01 us  [gather_weights(): from_left = lax.ppermute(w, 'x', right)]
    ppermute x1, waiting for transfers between devices: 0.01 us -> 5.8 us  [gather_weights(): w_y = lax.ppermute(w, 'yhi', SWAP)]
    all_to_all x2, waiting for transfers between devices: 30.9 us -> 26.5 us  [backward_move(): x = lax.all_to_all(x, 'z', 2, 2, tiled=True)]
    reduce_scatter x1, waiting for transfers between devices: 5.07 us -> 0.79 us  [body(): lax.psum_scatter(lax.dot_general(grads_in, hidden, (((0,), (0,)), ((), ()...]
    unnamed x30 -> x24, local copies, waits for them, and re-layouts: 5.96 us -> 2.47 us
  transfers between devices with their start and end apart: 20 -> 21, of which waited for: 12 -> 15; matrix products, arithmetic and copies ran while one was open for 12% -> 15% of each run, Pallas kernels for 0% -> 0%
where the time goes in v4:
time: 284 us; the launch traced here: 283 us
  waiting for transfers between devices  127 us (45%)
  starting transfers between devices  86.2 us (30%)
  local copies, waits for them, and re-layouts  26.7 us (9%)
  matrix products  22 us (8%)
  between operations  14.7 us (5%)
  other arithmetic  5.78 us (2%)
    ppermute x8, waiting for transfers between devices, swap_half(): got = lax.ppermute(go, axis_name, SWAP)  52.8 us
    all_to_all x2, waiting for transfers between devices, forward_move(): x = lax.all_to_all(x, 'z', 2, 2, tiled=True)  36.7 us
    all_to_all x2, waiting for transfers between devices, backward_move(): x = lax.all_to_all(x, 'z', 2, 2, tiled=True)  26.5 us
    all_to_all x2, starting transfers between devices, forward_move(): x = lax.all_to_all(x, 'z', 2, 2, tiled=True)  21.5 us
    all_to_all x2, starting transfers between devices, backward_move(): x = lax.all_to_all(x, 'z', 2, 2, tiled=True)  19.3 us
    ppermute x8, starting transfers between devices, swap_half(): got = lax.ppermute(go, axis_name, SWAP)  19.1 us
    dynamic_update_slice x8, local copies, waits for them, and re-layouts, gather_weights(): full = lax.dynamic_update_slice(full, piece, (0, owner * rows, 0))  9.28 us
    ppermute x1, waiting for transfers between devices, gather_weights(): w_y = lax.ppermute(w, 'yhi', SWAP)  5.8 us
  transfers between devices with their start and end apart: 21, of which 15 were waited for; matrix products, arithmetic and copies ran while one was open for 15% of the time, Pallas kernels for 0%

profile of v4, /device:TPU:6, one launch (start us, length us, event | category | flops | bytes accessed | tf_op | source)
XLA Modules:
  0.0 282.6 jit_solution(12426856586396931868)
XLA Ops:
  7.2 2.2 pad_maximum_fusion.2
  9.9 0.6 reduce-window.6
  11.9 2.5 copy.106
  14.4 15.3 %all-to-all-start.1 = ((bf16[2,2,80,2048]{3,1,0,2:T(2,128)(2,1)}), bf16[2,2,80,2048]{3,1,0,2:T(2,128)(2,1)S(1)}, u32[]{:S(2)}, u32[]{:S(2)}) async-start(bf16[2,2,80,2048]{3,1,0,2:T(2,128)(2,1)} %copy.106), calls=%async_computation.1 | async-start | bytes 2621440 | tf_op jit(solution)/shard_map/all_to_all | solution.py:24
  30.8 1.9 collective-permute-start
  32.8 2.1 collective-permute-done
  34.9 3.5 %collective-permute-start.1 = (bf16[2,1,80,2048]{3,2,1,0:T(8,128)(2,1)S(1)}, bf16[2,1,80,2048]{3,2,1,0:T(8,128)(2,1)S(1)}, u32[]{:S(2)}, u32[]{:S(2)}) collective-permute-start(bf16[2,1,80,2048]{3,2,1,0:T(8,128)(2,1)S(1)} %get-tuple-element.9), channel_id=1, source_target_pairs={{0,32},{32,0},{1,33},{33,1},{2,34},{34,2},{3,35},{35,3},{4,36},{36... | collective-permute-start | bytes 1966088 | tf_op jit(solution)/shard_map/ppermute | solution.py:18
  38.4 20.6 %collective-permute-done.1 = bf16[2,1,80,2048]{3,2,1,0:T(8,128)(2,1)S(1)} collective-permute-done((bf16[2,1,80,2048]{3,2,1,0:T(8,128)(2,1)S(1)}, bf16[2,1,80,2048]{3,2,1,0:T(8,128)(2,1)S(1)}, u32[]{:S(2)}, u32[]{:S(2)}) %collective-permute-start.1) | collective-permute-done | bytes 655392 | tf_op jit(solution)/shard_map/ppermute | solution.py:18
  59.2 2.4 copy.104
  61.6 31.0 %all-to-all-done.1 = bf16[2,2,80,2048]{3,1,0,2:T(2,128)(2,1)S(1)} async-done(((bf16[2,2,80,2048]{3,1,0,2:T(2,128)(2,1)}), bf16[2,2,80,2048]{3,1,0,2:T(2,128)(2,1)S(1)}, u32[]{:S(2)}, u32[]{:S(2)}) %all-to-all-start.1) | async-done | bytes 1310752 | tf_op jit(solution)/shard_map/all_to_all | solution.py:24
  92.6 6.2 %all-to-all-start = ((bf16[2,2,80,2048]{3,1,0,2:T(2,128)(2,1)}), bf16[2,2,80,2048]{3,1,0,2:T(2,128)(2,1)S(1)}, u32[]{:S(2)}, u32[]{:S(2)}) async-start(bf16[2,2,80,2048]{3,1,0,2:T(2,128)(2,1)} %copy.104), calls=%async_computation | async-start | bytes 2621440 | tf_op jit(solution)/shard_map/all_to_all | solution.py:28
  98.9 5.1 %collective-permute-start.2 = (bf16[1,256,768]{2,1,0:T(8,128)(2,1)}, bf16[1,256,768]{2,1,0:T(8,128)(2,1)}, u32[]{:S(2)}, u32[]{:S(2)}) collective-permute-start(bf16[1,256,768]{2,1,0:T(8,128)(2,1)} %param.13), channel_id=1, source_target_pairs={{0,64},{64,0},{1,65},{65,1},{2,66},{66,2},{3,67},{67,3},{4,68},{68... | collective-permute-start | bytes 1179656 | tf_op jit(solution)/shard_map/ppermute | solution.py:49
  104.0 2.7 collective-permute-start.4
  106.7 4.3 %collective-permute-start.3 = (bf16[1,256,768]{2,1,0:T(8,128)(2,1)}, bf16[1,256,768]{2,1,0:T(8,128)(2,1)}, u32[]{:S(2)}, u32[]{:S(2)}) collective-permute-start(bf16[1,256,768]{2,1,0:T(8,128)(2,1)} %param.13), channel_id=1, source_target_pairs={{0,128},{128,256},{256,384},{384,0},{1,129},{129,257},{257,385},{3... | collective-permute-start | bytes 1179656 | tf_op jit(solution)/shard_map/ppermute | solution.py:50
  111.2 1.9 squeeze.25
  113.1 0.8 bitcast_dynamic-update-slice_fusion.7
  113.8 5.8 %collective-permute-done.2 = bf16[1,256,768]{2,1,0:T(8,128)(2,1)} collective-permute-done((bf16[1,256,768]{2,1,0:T(8,128)(2,1)}, bf16[1,256,768]{2,1,0:T(8,128)(2,1)}, u32[]{:S(2)}, u32[]{:S(2)}) %collective-permute-start.2) | collective-permute-done | bytes 393248 | tf_op jit(solution)/shard_map/ppermute | solution.py:49
  119.6 2.4 collective-permute-start.5
  122.1 3.4 %collective-permute-start.6 = (bf16[1,256,768]{2,1,0:T(8,128)(2,1)}, bf16[1,256,768]{2,1,0:T(8,128)(2,1)S(1)}, u32[]{:S(2)}, u32[]{:S(2)}) collective-permute-start(bf16[1,256,768]{2,1,0:T(8,128)(2,1)} %collective-permute-done.2), channel_id=1, source_target_pairs={{0,384},{128,0},{256,128},{384,256},{1,385},{129,1},{257,129},{385... | collective-permute-start | bytes 1179656 | tf_op jit(solution)/shard_map/ppermute | solution.py:53
  125.5 2.8 collective-permute-start.7
  128.3 1.8 bitcast_dynamic-update-slice_fusion.6
  130.1 1.8 bitcast_dynamic-update-slice_fusion.5
  131.8 1.8 bitcast_dynamic-update-slice_fusion.4
  133.6 4.5 %collective-permute-done.5 = bf16[1,256,768]{2,1,0:T(8,128)(2,1)S(1)} collective-permute-done((bf16[1,256,768]{2,1,0:T(8,128)(2,1)}, bf16[1,256,768]{2,1,0:T(8,128)(2,1)S(1)}, u32[]{:S(2)}, u32[]{:S(2)}) %collective-permute-start.5) | collective-permute-done | bytes 393248 | tf_op jit(solution)/shard_map/ppermute | solution.py:52
  138.1 5.5 %collective-permute-start.8 = (bf16[1,256,768]{2,1,0:T(8,128)(2,1)S(1)}, bf16[1,256,768]{2,1,0:T(8,128)(2,1)S(1)}, u32[]{:S(2)}, u32[]{:S(2)}) collective-permute-start(bf16[1,256,768]{2,1,0:T(8,128)(2,1)S(1)} %collective-permute-done.5), channel_id=1, source_target_pairs={{0,128},{128,256},{256,384},{384,0},{1,129},{129,257},{257,385},{3... | collective-permute-start | bytes 1179656 | tf_op jit(solution)/shard_map/ppermute | solution.py:55
  143.6 0.9 fusion.38
  144.8 1.9 collective-permute-start.9
  146.7 0.8 bitcast_dynamic-update-slice_fusion.3
  147.7 1.1 collective-permute-done.9
  148.9 2.8 collective-permute-start.10
  151.7 0.8 bitcast_dynamic-update-slice_fusion.2
  152.5 0.8 bitcast_dynamic-update-slice_fusion.1
  153.3 0.8 bitcast_dynamic-update-slice_fusion
  154.1 5.7 %all-to-all-done = bf16[2,2,80,2048]{3,1,0,2:T(2,128)(2,1)S(1)} async-done(((bf16[2,2,80,2048]{3,1,0,2:T(2,128)(2,1)}), bf16[2,2,80,2048]{3,1,0,2:T(2,128)(2,1)S(1)}, u32[]{:S(2)}, u32[]{:S(2)}) %all-to-all-start) | async-done | bytes 1310752 | tf_op jit(solution)/shard_map/all_to_all | solution.py:28
  159.8 1.8 copy.105
  161.6 6.1 %collective-permute-done.10 = bf16[2,1,80,2048]{3,2,1,0:T(8,128)(2,1)} collective-permute-done((bf16[2,1,80,2048]{3,2,1,0:T(8,128)(2,1)S(1)}, bf16[2,1,80,2048]{3,2,1,0:T(8,128)(2,1)}, u32[]{:S(2)}, u32[]{:S(2)}) %collective-permute-start.10) | collective-permute-done | bytes 655392 | tf_op jit(solution)/shard_map/ppermute | solution.py:18
  167.7 1.2 pad_maximum_fusion.1
  168.9 3.2 %fusion = f32[320,768]{1,0:T(8,128)S(1)} fusion(bf16[320,2048]{1,0:T(8,128)(2,1)S(1)} %bitcast.96, bf16[2,2048,768]{2,1,0:T(8,128)(2,1)} %all-gather.2.cloned.1.call-done), kind=kOutput, calls=%fused_computation.2 | convolution fusion | flops 1006632960 | bytes 5439488 | tf_op jit(solution)/shard_map/dot_general | solution.py:100
  172.1 0.5 copy-done.1
  172.7 1.2 fusion.1
  173.9 0.9 copy-done.8
  174.8 3.7 %convolution_convert_fusion = bf16[2048,768]{1,0:T(8,128)(2,1)} fusion(bf16[320,2048]{1,0:T(8,128)(2,1)S(1)} %bitcast.94, f32[320,768]{1,0:T(8,128)S(1)} %fusion.1, f32[320,768]{1,0:T(8,128)S(1)} %fusion), kind=kOutput, calls=%fused_computation | convolution fusion | flops 1009680384 | bytes 6422528 | tf_op jit(solution)/shard_map/dot_general | solution.py:130
  178.5 3.8 %multiply_convert_fusion.2 = (bf16[320,768]{1,0:T(8,128)(2,1)S(1)}, bf16[320,768]{1,0:T(8,128)(2,1)S(1)}) fusion(f32[320,768]{1,0:T(8,128)} %copy-done.7, f32[320,768]{1,0:T(8,128)} %copy-done.8, bf16[320,2048]{1,0:T(8,128)(2,1)S(1)} %bitcast.95, bf16[2048,768]{1,0:T(8,128)(2,1)} %bitcast_dynamic-update-slice_fusion), kind=kOutput, calls=%fused_computation.28 | convolution fusion | flops 1009827840 | bytes 7405568 | tf_op jit(solution)/shard_map/dot_general | solution.py:105
  182.3 2.1 fusion.5
  184.4 2.1 fusion.10
  186.6 1.5 copy.109
  188.1 11.7 %all-to-all-start.2 = ((bf16[2,2,80,1024]{3,1,0,2:T(2,128)(2,1)}), bf16[2,2,80,1024]{3,1,0,2:T(2,128)(2,1)S(1)}, u32[]{:S(2)}, u32[]{:S(2)}) async-start(bf16[2,2,80,1024]{3,1,0,2:T(2,128)(2,1)} %copy.109), calls=%async_computation.2 | async-start | bytes 1310720 | tf_op jit(solution)/shard_map/all_to_all | solution.py:34
  199.8 2.1 fusion.3
  201.9 2.1 fusion.9
  204.1 2.6 collective-permute-start.13
  206.7 11.6 %collective-permute-done.13 = bf16[2,1,80,1024]{3,2,1,0:T(8,128)(2,1)S(1)} collective-permute-done((bf16[2,1,80,1024]{3,2,1,0:T(8,128)(2,1)S(1)}, bf16[2,1,80,1024]{3,2,1,0:T(8,128)(2,1)S(1)}, u32[]{:S(2)}, u32[]{:S(2)}) %collective-permute-start.13) | collective-permute-done | bytes 327712 | tf_op jit(solution)/shard_map/ppermute | solution.py:18
  218.4 1.9 collective-permute-start.14
  220.4 1.6 collective-permute-done.14
  222.0 1.5 copy.112
  223.5 9.2 %all-to-all-done.2 = bf16[2,2,80,1024]{3,1,0,2:T(2,128)(2,1)S(1)} async-done(((bf16[2,2,80,1024]{3,1,0,2:T(2,128)(2,1)}), bf16[2,2,80,1024]{3,1,0,2:T(2,128)(2,1)S(1)}, u32[]{:S(2)}, u32[]{:S(2)}) %all-to-all-start.2) | async-done | bytes 655392 | tf_op jit(solution)/shard_map/all_to_all | solution.py:34
  232.8 7.5 %all-to-all-start.3 = ((bf16[2,2,80,1024]{3,1,0,2:T(2,128)(2,1)}), bf16[2,2,80,1024]{3,1,0,2:T(2,128)(2,1)S(1)}, u32[]{:S(2)}, u32[]{:S(2)}) async-start(bf16[2,2,80,1024]{3,1,0,2:T(2,128)(2,1)} %copy.112), calls=%async_computation.3 | async-start | bytes 1310720 | tf_op jit(solution)/shard_map/all_to_all | solution.py:38
  240.3 0.9 fusion.41
  241.4 2.6 collective-permute-start.11
  244.2 8.1 %collective-permute-done.11 = bf16[2,1,80,1024]{3,2,1,0:T(8,128)(2,1)S(1)} collective-permute-done((bf16[2,1,80,1024]{3,2,1,0:T(8,128)(2,1)S(1)}, bf16[2,1,80,1024]{3,2,1,0:T(8,128)(2,1)S(1)}, u32[]{:S(2)}, u32[]{:S(2)}) %collective-permute-start.11) | collective-permute-done | bytes 327712 | tf_op jit(solution)/shard_map/ppermute | solution.py:18
  252.4 1.9 collective-permute-start.12
  254.3 1.6 collective-permute-done.12
  256.3 17.3 %all-to-all-done.3 = bf16[2,2,80,1024]{3,1,0,2:T(2,128)(2,1)S(1)} async-done(((bf16[2,2,80,1024]{3,1,0,2:T(2,128)(2,1)}), bf16[2,2,80,1024]{3,1,0,2:T(2,128)(2,1)S(1)}, u32[]{:S(2)}, u32[]{:S(2)}) %all-to-all-start.3) | async-done | bytes 655392 | tf_op jit(solution)/shard_map/all_to_all | solution.py:38
  274.1 0.8 pad_maximum_fusion.6
  275.0 0.8 reduce-scatter.2.cloned.1.call-done
  (64 shorter events, 5.3 us)
Async XLA Ops:
  7.2 4.2 %copy-start = (bf16[128,2048]{1,0:T(8,128)(2,1)S(1)}, bf16[128,2048]{1,0:T(8,128)(2,1)}, u32[]{:S(2)}) copy-start(bf16[128,2048]{1,0:T(8,128)(2,1)} %param.7) | copy-start | bytes 1572868
  7.2 2.3 copy-start.5
  7.2 161.7 %all-gather.2.cloned.1.call-start = ((), (), s32[]{:S(2)}) async-start(), calls=%async_computation.5 | async-start | bytes 7077888 | tf_op jit(solution)/shard_map/all_gather | solution.py:75
  14.4 15.3 %copy-start.6 = (f32[128,2]{0,1:T(2,128)S(1)}, f32[128,2]{0,1:T(2,128)}, u32[]{:S(2)}) copy-start(f32[128,2]{0,1:T(2,128)} %param.9) | copy-start | bytes 3076
  14.4 15.8 %copy-start.3 = (bf16[128,2048]{1,0:T(8,128)(2,1)S(1)}, bf16[128,2048]{1,0:T(8,128)(2,1)}, u32[]{:S(2)}) copy-start(bf16[128,2048]{1,0:T(8,128)(2,1)} %param.8) | copy-start | bytes 1572868
  14.4 78.2 %all-to-all-start.1 = ((bf16[2,2,80,2048]{3,1,0,2:T(2,128)(2,1)}), bf16[2,2,80,2048]{3,1,0,2:T(2,128)(2,1)S(1)}, u32[]{:S(2)}, u32[]{:S(2)}) async-start(bf16[2,2,80,2048]{3,1,0,2:T(2,128)(2,1)} %copy.106), calls=%async_computation.1 | async-start | bytes 2621440 | tf_op jit(solution)/shard_map/all_to_all | solution.py:24
  30.8 4.0 %collective-permute-start = (bf16[1,2,80,2048]{3,2,1,0:T(8,128)(2,1)S(1)}, bf16[1,2,80,2048]{3,2,1,0:T(8,128)(2,1)S(1)}, u32[]{:S(2)}, u32[]{:S(2)}) collective-permute-start(bf16[1,2,80,2048]{3,2,1,0:T(8,128)(2,1)S(1)} %bitcast.98), channel_id=1, source_target_pairs={{0,1},{1,0},{2,3},{3,2},{4,5},{5,4},{6,7},{7,6},{8,9},{9,8},{10,11... | collective-permute-start | bytes 1966088 | tf_op jit(solution)/shard_map/ppermute | solution.py:18
  34.9 24.1 %collective-permute-start.1 = (bf16[2,1,80,2048]{3,2,1,0:T(8,128)(2,1)S(1)}, bf16[2,1,80,2048]{3,2,1,0:T(8,128)(2,1)S(1)}, u32[]{:S(2)}, u32[]{:S(2)}) collective-permute-start(bf16[2,1,80,2048]{3,2,1,0:T(8,128)(2,1)S(1)} %get-tuple-element.9), channel_id=1, source_target_pairs={{0,32},{32,0},{1,33},{33,1},{2,34},{34,2},{3,35},{35,3},{4,36},{36... | collective-permute-start | bytes 1966088 | tf_op jit(solution)/shard_map/ppermute | solution.py:18
  92.6 67.2 %all-to-all-start = ((bf16[2,2,80,2048]{3,1,0,2:T(2,128)(2,1)}), bf16[2,2,80,2048]{3,1,0,2:T(2,128)(2,1)S(1)}, u32[]{:S(2)}, u32[]{:S(2)}) async-start(bf16[2,2,80,2048]{3,1,0,2:T(2,128)(2,1)} %copy.104), calls=%async_computation | async-start | bytes 2621440 | tf_op jit(solution)/shard_map/all_to_all | solution.py:28
  98.8 176.9 %reduce-scatter.2.cloned.1.call-start = ((), (), s32[]{:S(2)}) async-start(), calls=%async_computation.6 | async-start | bytes 3538944 | tf_op jit(solution)/shard_map/reduce_scatter | solution.py:129
  98.9 20.8 %collective-permute-start.2 = (bf16[1,256,768]{2,1,0:T(8,128)(2,1)}, bf16[1,256,768]{2,1,0:T(8,128)(2,1)}, u32[]{:S(2)}, u32[]{:S(2)}) collective-permute-start(bf16[1,256,768]{2,1,0:T(8,128)(2,1)} %param.13), channel_id=1, source_target_pairs={{0,64},{64,0},{1,65},{65,1},{2,66},{66,2},{3,67},{67,3},{4,68},{68... | collective-permute-start | bytes 1179656 | tf_op jit(solution)/shard_map/ppermute | solution.py:49
  104.0 21.5 %collective-permute-start.4 = (bf16[1,256,768]{2,1,0:T(8,128)(2,1)}, bf16[1,256,768]{2,1,0:T(8,128)(2,1)}, u32[]{:S(2)}, u32[]{:S(2)}) collective-permute-start(bf16[1,256,768]{2,1,0:T(8,128)(2,1)} %param.13), channel_id=1, source_target_pairs={{0,384},{128,0},{256,128},{384,256},{1,385},{129,1},{257,129},{385... | collective-permute-start | bytes 1179656 | tf_op jit(solution)/shard_map/ppermute | solution.py:51
  106.7 23.3 %collective-permute-start.3 = (bf16[1,256,768]{2,1,0:T(8,128)(2,1)}, bf16[1,256,768]{2,1,0:T(8,128)(2,1)}, u32[]{:S(2)}, u32[]{:S(2)}) collective-permute-start(bf16[1,256,768]{2,1,0:T(8,128)(2,1)} %param.13), channel_id=1, source_target_pairs={{0,128},{128,256},{256,384},{384,0},{1,129},{129,257},{257,385},{3... | collective-permute-start | bytes 1179656 | tf_op jit(solution)/shard_map/ppermute | solution.py:50
  111.2 1.9 copy-start.4
  119.6 18.5 %collective-permute-start.5 = (bf16[1,256,768]{2,1,0:T(8,128)(2,1)}, bf16[1,256,768]{2,1,0:T(8,128)(2,1)S(1)}, u32[]{:S(2)}, u32[]{:S(2)}) collective-permute-start(bf16[1,256,768]{2,1,0:T(8,128)(2,1)} %collective-permute-done.2), channel_id=1, source_target_pairs={{0,128},{128,256},{256,384},{384,0},{1,129},{129,257},{257,385},{3... | collective-permute-start | bytes 1179656 | tf_op jit(solution)/shard_map/ppermute | solution.py:52
  122.1 29.6 %collective-permute-start.6 = (bf16[1,256,768]{2,1,0:T(8,128)(2,1)}, bf16[1,256,768]{2,1,0:T(8,128)(2,1)S(1)}, u32[]{:S(2)}, u32[]{:S(2)}) collective-permute-start(bf16[1,256,768]{2,1,0:T(8,128)(2,1)} %collective-permute-done.2), channel_id=1, source_target_pairs={{0,384},{128,0},{256,128},{384,256},{1,385},{129,1},{257,129},{385... | collective-permute-start | bytes 1179656 | tf_op jit(solution)/shard_map/ppermute | solution.py:53
  125.5 27.0 %collective-permute-start.7 = (bf16[1,256,768]{2,1,0:T(8,128)(2,1)}, bf16[1,256,768]{2,1,0:T(8,128)(2,1)S(1)}, u32[]{:S(2)}, u32[]{:S(2)}) collective-permute-start(bf16[1,256,768]{2,1,0:T(8,128)(2,1)} %collective-permute-done.4), channel_id=1, source_target_pairs={{0,384},{128,0},{256,128},{384,256},{1,385},{129,1},{257,129},{385... | collective-permute-start | bytes 1179656 | tf_op jit(solution)/shard_map/ppermute | solution.py:54
  138.1 15.1 %collective-permute-start.8 = (bf16[1,256,768]{2,1,0:T(8,128)(2,1)S(1)}, bf16[1,256,768]{2,1,0:T(8,128)(2,1)S(1)}, u32[]{:S(2)}, u32[]{:S(2)}) collective-permute-start(bf16[1,256,768]{2,1,0:T(8,128)(2,1)S(1)} %collective-permute-done.5), channel_id=1, source_target_pairs={{0,128},{128,256},{256,384},{384,0},{1,129},{129,257},{257,385},{3... | collective-permute-start | bytes 1179656 | tf_op jit(solution)/shard_map/ppermute | solution.py:55
  144.8 4.0 %collective-permute-start.9 = (bf16[1,2,80,2048]{3,2,1,0:T(8,128)(2,1)S(1)}, bf16[1,2,80,2048]{3,2,1,0:T(8,128)(2,1)S(1)}, u32[]{:S(2)}, u32[]{:S(2)}) collective-permute-start(bf16[1,2,80,2048]{3,2,1,0:T(8,128)(2,1)S(1)} %copy.115), channel_id=1, source_target_pairs={{0,1},{1,0},{2,3},{3,2},{4,5},{5,4},{6,7},{7,6},{8,9},{9,8},{10,11... | collective-permute-start | bytes 1966088 | tf_op jit(solution)/shard_map/ppermute | solution.py:18
  148.9 18.8 %collective-permute-start.10 = (bf16[2,1,80,2048]{3,2,1,0:T(8,128)(2,1)S(1)}, bf16[2,1,80,2048]{3,2,1,0:T(8,128)(2,1)}, u32[]{:S(2)}, u32[]{:S(2)}) collective-permute-start(bf16[2,1,80,2048]{3,2,1,0:T(8,128)(2,1)S(1)} %get-tuple-element.5), channel_id=1, source_target_pairs={{0,32},{32,0},{1,33},{33,1},{2,34},{34,2},{3,35},{35,3},{4,36},{36... | collective-permute-start | bytes 1966088 | tf_op jit(solution)/shard_map/ppermute | solution.py:18
  168.9 3.7 %copy-start.1 = (bf16[2,2048,768]{2,1,0:T(8,128)(2,1)S(1)}, bf16[2,2048,768]{2,1,0:T(8,128)(2,1)}, u32[]{:S(2)}) copy-start(bf16[2,2048,768]{2,1,0:T(8,128)(2,1)} %all-gather.2.cloned.1.call-done) | copy-start | bytes 18874372
  172.6 1.2 copy-start.7
  172.6 2.2 copy-start.2
  173.9 0.9 copy-start.8
  188.1 44.7 %all-to-all-start.2 = ((bf16[2,2,80,1024]{3,1,0,2:T(2,128)(2,1)}), bf16[2,2,80,1024]{3,1,0,2:T(2,128)(2,1)S(1)}, u32[]{:S(2)}, u32[]{:S(2)}) async-start(bf16[2,2,80,1024]{3,1,0,2:T(2,128)(2,1)} %copy.109), calls=%async_computation.2 | async-start | bytes 1310720 | tf_op jit(solution)/shard_map/all_to_all | solution.py:34
  204.1 14.2 %collective-permute-start.13 = (bf16[2,1,80,1024]{3,2,1,0:T(8,128)(2,1)S(1)}, bf16[2,1,80,1024]{3,2,1,0:T(8,128)(2,1)S(1)}, u32[]{:S(2)}, u32[]{:S(2)}) collective-permute-start(bf16[2,1,80,1024]{3,2,1,0:T(8,128)(2,1)S(1)} %get-tuple-element.19), channel_id=1, source_target_pairs={{0,32},{32,0},{1,33},{33,1},{2,34},{34,2},{3,35},{35,3},{4,36},{36... | collective-permute-start | bytes 983048 | tf_op jit(solution)/shard_map/ppermute | solution.py:18
  218.4 3.5 %collective-permute-start.14 = (bf16[1,2,80,1024]{3,2,1,0:T(8,128)(2,1)S(1)}, bf16[1,2,80,1024]{3,2,1,0:T(8,128)(2,1)S(1)}, u32[]{:S(2)}, u32[]{:S(2)}) collective-permute-start(bf16[1,2,80,1024]{3,2,1,0:T(8,128)(2,1)S(1)} %get-tuple-element.17), channel_id=1, source_target_pairs={{0,1},{1,0},{2,3},{3,2},{4,5},{5,4},{6,7},{7,6},{8,9},{9,8},{10,11... | collective-permute-start | bytes 983048 | tf_op jit(solution)/shard_map/ppermute | solution.py:18
  232.8 40.8 %all-to-all-start.3 = ((bf16[2,2,80,1024]{3,1,0,2:T(2,128)(2,1)}), bf16[2,2,80,1024]{3,1,0,2:T(2,128)(2,1)S(1)}, u32[]{:S(2)}, u32[]{:S(2)}) async-start(bf16[2,2,80,1024]{3,1,0,2:T(2,128)(2,1)} %copy.112), calls=%async_computation.3 | async-start | bytes 1310720 | tf_op jit(solution)/shard_map/all_to_all | solution.py:38
  241.4 10.9 %collective-permute-start.11 = (bf16[2,1,80,1024]{3,2,1,0:T(8,128)(2,1)S(1)}, bf16[2,1,80,1024]{3,2,1,0:T(8,128)(2,1)S(1)}, u32[]{:S(2)}, u32[]{:S(2)}) collective-permute-start(bf16[2,1,80,1024]{3,2,1,0:T(8,128)(2,1)S(1)} %copy.117), channel_id=1, source_target_pairs={{0,32},{32,0},{1,33},{33,1},{2,34},{34,2},{3,35},{35,3},{4,36},{36... | collective-permute-start | bytes 983048 | tf_op jit(solution)/shard_map/ppermute | solution.py:18
  252.4 3.5 %collective-permute-start.12 = (bf16[1,2,80,1024]{3,2,1,0:T(8,128)(2,1)S(1)}, bf16[1,2,80,1024]{3,2,1,0:T(8,128)(2,1)S(1)}, u32[]{:S(2)}, u32[]{:S(2)}) collective-permute-start(bf16[1,2,80,1024]{3,2,1,0:T(8,128)(2,1)S(1)} %get-tuple-element.13), channel_id=1, source_target_pairs={{0,1},{1,0},{2,3},{3,2},{4,5},{5,4},{6,7},{7,6},{8,9},{9,8},{10,11... | collective-permute-start | bytes 983048 | tf_op jit(solution)/shard_map/ppermute | solution.py:18
Sparse Core Ops, SparseCore 0:
  11.2 126.0 all-gather.1
  178.7 97.0 reduce-scatter.1

commit v5 on v4

--- a/solution.py
+++ b/solution.py
@@ -126,13 +126,17 @@
             ).astype(jnp.bfloat16)
         )
     token_grad = jnp.concatenate(pieces, 1)
+    down_term = lax.dot_general(
+        grads_in, hidden, (((0,), (0,)), ((), ())), preferred_element_type=jnp.float32
+    ).astype(jnp.bfloat16)
+    n_x = lax.axis_size("x")
+    y_i = lax.axis_index("yhi")
+    blocks = down_term.reshape(n_x, 2, -1, down_term.shape[1])
+    keep = lax.dynamic_index_in_dim(blocks, y_i, axis=1, keepdims=False)
+    got = lax.ppermute(lax.dynamic_index_in_dim(blocks, 1 - y_i, axis=1, keepdims=False), "yhi", SWAP)
+    pair = (keep.astype(jnp.float32) + got.astype(jnp.float32)).astype(jnp.bfloat16)
     down_grad = lax.psum_scatter(
-        lax.dot_general(
-            grads_in, hidden, (((0,), (0,)), ((), ())), preferred_element_type=jnp.float32
-        ).astype(jnp.bfloat16),
-        DP,
-        scatter_dimension=0,
-        tiled=True,
+        pair.reshape(-1, down_term.shape[1]), "x", scatter_dimension=0, tiled=True
     )
     return (token_grad, down_grad[None])
 

time: 284 us -> 312 us (1.099)
  waiting for transfers between devices: 127 us -> 139 us
  starting transfers between devices: 86.2 us -> 94 us
  other arithmetic: 5.78 us -> 13.1 us
    ppermute x8, waiting for transfers between devices: 52.8 us -> 73.2 us  [swap_half(): got = lax.ppermute(go, axis_name, SWAP)]
    all_to_all x2, waiting for transfers between devices: 26.5 us -> 19 us  [backward_move(): x = lax.all_to_all(x, 'z', 2, 2, tiled=True)]
    all_to_all x2, starting transfers between devices: 19.3 us -> 23.5 us  [backward_move(): x = lax.all_to_all(x, 'z', 2, 2, tiled=True)]
    concatenate x6, other arithmetic: 1.62 us -> 5.53 us  [swap_half(): return jnp.concatenate([stay, got], dim)]
    convert_element_type x0 -> x1, other arithmetic: none -> 3.45 us  [body(): (keep.astype(jnp.float32) + got.astype(jnp.float32)).astype(jnp.bfloat16)]
  transfers between devices with their start and end apart: 21 -> 22, of which waited for: 15 -> 12; matrix products, arithmetic and copies ran while one was open for 15% -> 14% of each run, Pallas kernels for 0% -> 0%
where the time goes in v5:
time: 312 us; the launch traced here: 311 us
  waiting for transfers between devices  139 us (45%)
  starting transfers between devices  94 us (30%)
  local copies, waits for them, and re-layouts  29 us (9%)
  matrix products  20.8 us (7%)
  between operations  14.7 us (5%)
  other arithmetic  13.1 us (4%)
    ppermute x8, waiting for transfers between devices, swap_half(): got = lax.ppermute(go, axis_name, SWAP)  73.2 us
    all_to_all x2, waiting for transfers between devices, forward_move(): x = lax.all_to_all(x, 'z', 2, 2, tiled=True)  36.7 us
    all_to_all x2, starting transfers between devices, backward_move(): x = lax.all_to_all(x, 'z', 2, 2, tiled=True)  23.5 us
    all_to_all x2, starting transfers between devices, forward_move(): x = lax.all_to_all(x, 'z', 2, 2, tiled=True)  21.5 us
    ppermute x8, starting transfers between devices, swap_half(): got = lax.ppermute(go, axis_name, SWAP)  20.1 us
    all_to_all x2, waiting for transfers between devices, backward_move(): x = lax.all_to_all(x, 'z', 2, 2, tiled=True)  19 us
    dynamic_update_slice x8, local copies, waits for them, and re-layouts, gather_weights(): full = lax.dynamic_update_slice(full, piece, (0, owner * rows, 0))  9.32 us
  transfers between devices with their start and end apart: 22, of which 12 were waited for; matrix products, arithmetic and copies ran while one was open for 14% of the time, Pallas kernels for 0%

profile of v5, /device:TPU:6, one launch (start us, length us, event | category | flops | bytes accessed | tf_op | source)
XLA Modules:
  0.0 311.0 jit_solution(12156257803602461448)
XLA Ops:
  7.2 2.2 pad_maximum_fusion.2
  11.9 2.4 copy.106
  14.3 15.3 %all-to-all-start.1 = ((bf16[2,2,80,2048]{3,1,0,2:T(2,128)(2,1)}), bf16[2,2,80,2048]{3,1,0,2:T(2,128)(2,1)S(1)}, u32[]{:S(2)}, u32[]{:S(2)}) async-start(bf16[2,2,80,2048]{3,1,0,2:T(2,128)(2,1)} %copy.106), calls=%async_computation.1 | async-start | bytes 2621440 | tf_op jit(solution)/shard_map/all_to_all | solution.py:24
  30.7 1.9 collective-permute-start
  32.7 2.1 collective-permute-done
  34.8 3.5 %collective-permute-start.1 = (bf16[2,1,80,2048]{3,2,1,0:T(8,128)(2,1)S(1)}, bf16[2,1,80,2048]{3,2,1,0:T(8,128)(2,1)S(1)}, u32[]{:S(2)}, u32[]{:S(2)}) collective-permute-start(bf16[2,1,80,2048]{3,2,1,0:T(8,128)(2,1)S(1)} %get-tuple-element.9), channel_id=1, source_target_pairs={{0,32},{32,0},{1,33},{33,1},{2,34},{34,2},{3,35},{35,3},{4,36},{36... | collective-permute-start | bytes 1966088 | tf_op jit(solution)/shard_map/ppermute | solution.py:18
  38.3 20.7 %collective-permute-done.1 = bf16[2,1,80,2048]{3,2,1,0:T(8,128)(2,1)S(1)} collective-permute-done((bf16[2,1,80,2048]{3,2,1,0:T(8,128)(2,1)S(1)}, bf16[2,1,80,2048]{3,2,1,0:T(8,128)(2,1)S(1)}, u32[]{:S(2)}, u32[]{:S(2)}) %collective-permute-start.1) | collective-permute-done | bytes 655392 | tf_op jit(solution)/shard_map/ppermute | solution.py:18
  59.2 2.4 copy.104
  61.6 30.9 %all-to-all-done.1 = bf16[2,2,80,2048]{3,1,0,2:T(2,128)(2,1)S(1)} async-done(((bf16[2,2,80,2048]{3,1,0,2:T(2,128)(2,1)}), bf16[2,2,80,2048]{3,1,0,2:T(2,128)(2,1)S(1)}, u32[]{:S(2)}, u32[]{:S(2)}) %all-to-all-start.1) | async-done | bytes 1310752 | tf_op jit(solution)/shard_map/all_to_all | solution.py:24
  92.5 6.2 %all-to-all-start = ((bf16[2,2,80,2048]{3,1,0,2:T(2,128)(2,1)}), bf16[2,2,80,2048]{3,1,0,2:T(2,128)(2,1)S(1)}, u32[]{:S(2)}, u32[]{:S(2)}) async-start(bf16[2,2,80,2048]{3,1,0,2:T(2,128)(2,1)} %copy.104), calls=%async_computation | async-start | bytes 2621440 | tf_op jit(solution)/shard_map/all_to_all | solution.py:28
  98.7 5.1 %collective-permute-start.2 = (bf16[1,256,768]{2,1,0:T(8,128)(2,1)}, bf16[1,256,768]{2,1,0:T(8,128)(2,1)}, u32[]{:S(2)}, u32[]{:S(2)}) collective-permute-start(bf16[1,256,768]{2,1,0:T(8,128)(2,1)} %param.13), channel_id=1, source_target_pairs={{0,64},{64,0},{1,65},{65,1},{2,66},{66,2},{3,67},{67,3},{4,68},{68... | collective-permute-start | bytes 1179656 | tf_op jit(solution)/shard_map/ppermute | solution.py:49
  103.8 2.7 collective-permute-start.4
  106.6 4.3 %collective-permute-start.3 = (bf16[1,256,768]{2,1,0:T(8,128)(2,1)}, bf16[1,256,768]{2,1,0:T(8,128)(2,1)}, u32[]{:S(2)}, u32[]{:S(2)}) collective-permute-start(bf16[1,256,768]{2,1,0:T(8,128)(2,1)} %param.13), channel_id=1, source_target_pairs={{0,128},{128,256},{256,384},{384,0},{1,129},{129,257},{257,385},{3... | collective-permute-start | bytes 1179656 | tf_op jit(solution)/shard_map/ppermute | solution.py:50
  111.0 1.9 squeeze.30
  112.9 0.8 bitcast_dynamic-update-slice_fusion.7
  113.8 6.0 %collective-permute-done.2 = bf16[1,256,768]{2,1,0:T(8,128)(2,1)} collective-permute-done((bf16[1,256,768]{2,1,0:T(8,128)(2,1)}, bf16[1,256,768]{2,1,0:T(8,128)(2,1)}, u32[]{:S(2)}, u32[]{:S(2)}) %collective-permute-start.2) | collective-permute-done | bytes 393248 | tf_op jit(solution)/shard_map/ppermute | solution.py:49
  119.7 2.4 collective-permute-start.5
  122.2 3.4 %collective-permute-start.6 = (bf16[1,256,768]{2,1,0:T(8,128)(2,1)}, bf16[1,256,768]{2,1,0:T(8,128)(2,1)S(1)}, u32[]{:S(2)}, u32[]{:S(2)}) collective-permute-start(bf16[1,256,768]{2,1,0:T(8,128)(2,1)} %collective-permute-done.2), channel_id=1, source_target_pairs={{0,384},{128,0},{256,128},{384,256},{1,385},{129,1},{257,129},{385... | collective-permute-start | bytes 1179656 | tf_op jit(solution)/shard_map/ppermute | solution.py:53
  125.6 2.8 collective-permute-start.7
  128.4 1.8 bitcast_dynamic-update-slice_fusion.6
  130.1 1.8 bitcast_dynamic-update-slice_fusion.5
  132.0 1.8 bitcast_dynamic-update-slice_fusion.4
  133.7 4.3 %collective-permute-done.5 = bf16[1,256,768]{2,1,0:T(8,128)(2,1)S(1)} collective-permute-done((bf16[1,256,768]{2,1,0:T(8,128)(2,1)}, bf16[1,256,768]{2,1,0:T(8,128)(2,1)S(1)}, u32[]{:S(2)}, u32[]{:S(2)}) %collective-permute-start.5) | collective-permute-done | bytes 393248 | tf_op jit(solution)/shard_map/ppermute | solution.py:52
  138.0 5.5 %collective-permute-start.8 = (bf16[1,256,768]{2,1,0:T(8,128)(2,1)S(1)}, bf16[1,256,768]{2,1,0:T(8,128)(2,1)S(1)}, u32[]{:S(2)}, u32[]{:S(2)}) collective-permute-start(bf16[1,256,768]{2,1,0:T(8,128)(2,1)S(1)} %collective-permute-done.5), channel_id=1, source_target_pairs={{0,128},{128,256},{256,384},{384,0},{1,129},{129,257},{257,385},{3... | collective-permute-start | bytes 1179656 | tf_op jit(solution)/shard_map/ppermute | solution.py:55
  143.5 0.9 fusion.39
  144.6 1.9 collective-permute-start.9
  146.5 0.8 bitcast_dynamic-update-slice_fusion.3
  147.5 1.0 collective-permute-done.9
  148.7 2.8 collective-permute-start.10
  151.5 0.8 bitcast_dynamic-update-slice_fusion.2
  152.3 0.8 bitcast_dynamic-update-slice_fusion.1
  153.1 0.8 bitcast_dynamic-update-slice_fusion
  153.9 5.8 %all-to-all-done = bf16[2,2,80,2048]{3,1,0,2:T(2,128)(2,1)S(1)} async-done(((bf16[2,2,80,2048]{3,1,0,2:T(2,128)(2,1)}), bf16[2,2,80,2048]{3,1,0,2:T(2,128)(2,1)S(1)}, u32[]{:S(2)}, u32[]{:S(2)}) %all-to-all-start) | async-done | bytes 1310752 | tf_op jit(solution)/shard_map/all_to_all | solution.py:28
  159.7 1.8 copy.105
  161.5 6.1 %collective-permute-done.10 = bf16[2,1,80,2048]{3,2,1,0:T(8,128)(2,1)} collective-permute-done((bf16[2,1,80,2048]{3,2,1,0:T(8,128)(2,1)S(1)}, bf16[2,1,80,2048]{3,2,1,0:T(8,128)(2,1)}, u32[]{:S(2)}, u32[]{:S(2)}) %collective-permute-start.10) | collective-permute-done | bytes 655392 | tf_op jit(solution)/shard_map/ppermute | solution.py:18
  167.5 2.3 pad_maximum_fusion.1
  169.8 3.6 %fusion = f32[320,768]{1,0:T(8,128)S(1)} fusion(bf16[320,2048]{1,0:T(8,128)(2,1)} %bitcast.13, bf16[2,2048,768]{2,1,0:T(8,128)(2,1)} %all-gather.2.cloned.1.call-done), kind=kOutput, calls=%fused_computation.2 | convolution fusion | flops 1006632960 | bytes 5439488 | tf_op jit(solution)/shard_map/dot_general | solution.py:100
  173.9 2.9 fusion.1
  176.9 3.6 %multiply_convert_fusion.2 = (bf16[320,768]{1,0:T(8,128)(2,1)S(1)}, bf16[320,768]{1,0:T(8,128)(2,1)S(1)}) fusion(f32[320,768]{1,0:T(8,128)S(1)} %fusion, f32[320,768]{1,0:T(8,128)S(1)} %fusion.1, bf16[320,2048]{1,0:T(8,128)(2,1)S(1)} %bitcast.104, bf16[2048,768]{1,0:T(8,128)(2,1)} %bitcast_dynamic-update-slice_fusion), kind=kOutput, calls=%fused_computation.31 | convolution fusion | flops 1009827840 | bytes 7405568 | tf_op jit(solution)/shard_map/dot_general | solution.py:105
  181.3 0.7 fusion.11
  182.0 1.5 copy.109
  183.5 11.7 %all-to-all-start.2 = ((bf16[2,2,80,1024]{3,1,0,2:T(2,128)(2,1)}), bf16[2,2,80,1024]{3,1,0,2:T(2,128)(2,1)S(1)}, u32[]{:S(2)}, u32[]{:S(2)}) async-start(bf16[2,2,80,1024]{3,1,0,2:T(2,128)(2,1)} %copy.109), calls=%async_computation.2 | async-start | bytes 1310720 | tf_op jit(solution)/shard_map/all_to_all | solution.py:34
  195.3 3.4 %convolution_convert_fusion = bf16[2048,768]{1,0:T(8,128)(2,1)S(1)} fusion(bf16[320,2048]{1,0:T(8,128)(2,1)S(1)} %bitcast.105, f32[320,768]{1,0:T(8,128)} %copy-done.12, f32[320,768]{1,0:T(8,128)} %copy-done.11), kind=kOutput, calls=%fused_computation | convolution fusion | flops 1009680384 | bytes 6422528 | tf_op jit(solution)/shard_map/dot_general | solution.py:129
  198.9 1.6 copy-done.1
  200.4 2.7 collective-permute-start.15
  203.1 2.1 fusion.4
  205.2 2.1 fusion.10
  207.4 0.9 fusion.43
  208.2 3.0 collective-permute-start.13
  211.3 33.3 %collective-permute-done.13 = bf16[2,1,80,1024]{3,2,1,0:T(8,128)(2,1)S(1)} collective-permute-done((bf16[2,1,80,1024]{3,2,1,0:T(8,128)(2,1)}, bf16[2,1,80,1024]{3,2,1,0:T(8,128)(2,1)S(1)}, u32[]{:S(2)}, u32[]{:S(2)}) %collective-permute-start.13) | collective-permute-done | bytes 327712 | tf_op jit(solution)/shard_map/ppermute | solution.py:18
  244.6 0.7 copy-done.6
  245.3 1.9 fusion.14
  247.2 1.9 collective-permute-start.14
  249.1 3.4 %fusion.2 = bf16[4,256,768]{2,1,0:T(8,128)(2,1)} fusion(bf16[4,256,768]{2,1,0:T(8,128)(2,1)} %collective-permute-done.15, bf16[4,2,256,768]{3,2,1,0:T(8,128)(2,1)} %bitcast.98, s32[]{:T(128)S(6)} %select_n.129), kind=kLoop, calls=%fused_computation.6 | loop fusion | flops 3145728 | bytes 4718596 | tf_op jit(solution)/shard_map/convert_element_type | solution.py:137
  252.6 1.0 pad_maximum_fusion.5
  253.7 1.5 copy.112
  255.2 11.7 %all-to-all-start.3 = ((bf16[2,2,80,1024]{3,1,0,2:T(2,128)(2,1)}), bf16[2,2,80,1024]{3,1,0,2:T(2,128)(2,1)S(1)}, u32[]{:S(2)}, u32[]{:S(2)}) async-start(bf16[2,2,80,1024]{3,1,0,2:T(2,128)(2,1)} %copy.112), calls=%async_computation.3 | async-start | bytes 1310720 | tf_op jit(solution)/shard_map/all_to_all | solution.py:38
  266.9 0.9 fusion.42
  268.0 3.1 %collective-permute-start.11 = (bf16[2,1,80,1024]{3,2,1,0:T(8,128)(2,1)S(1)}, bf16[2,1,80,1024]{3,2,1,0:T(8,128)(2,1)S(1)}, u32[]{:S(2)}, u32[]{:S(2)}) collective-permute-start(bf16[2,1,80,1024]{3,2,1,0:T(8,128)(2,1)S(1)} %copy.117), channel_id=1, source_target_pairs={{0,32},{32,0},{1,33},{33,1},{2,34},{34,2},{3,35},{35,3},{4,36},{36... | collective-permute-start | bytes 983048 | tf_op jit(solution)/shard_map/ppermute | solution.py:18
  271.3 8.4 %collective-permute-done.11 = bf16[2,1,80,1024]{3,2,1,0:T(8,128)(2,1)S(1)} collective-permute-done((bf16[2,1,80,1024]{3,2,1,0:T(8,128)(2,1)S(1)}, bf16[2,1,80,1024]{3,2,1,0:T(8,128)(2,1)S(1)}, u32[]{:S(2)}, u32[]{:S(2)}) %collective-permute-start.11) | collective-permute-done | bytes 327712 | tf_op jit(solution)/shard_map/ppermute | solution.py:18
  279.8 1.9 collective-permute-start.12
  281.8 1.6 collective-permute-done.12
  283.8 19.0 %all-to-all-done.3 = bf16[2,2,80,1024]{3,1,0,2:T(2,128)(2,1)S(1)} async-done(((bf16[2,2,80,1024]{3,1,0,2:T(2,128)(2,1)}), bf16[2,2,80,1024]{3,1,0,2:T(2,128)(2,1)S(1)}, u32[]{:S(2)}, u32[]{:S(2)}) %all-to-all-start.3) | async-done | bytes 655392 | tf_op jit(solution)/shard_map/all_to_all | solution.py:38
  303.3 0.8 pad_maximum_fusion.6
  (76 shorter events, 7.1 us)
Async XLA Ops:
  7.2 4.2 %copy-start = (bf16[128,2048]{1,0:T(8,128)(2,1)S(1)}, bf16[128,2048]{1,0:T(8,128)(2,1)}, u32[]{:S(2)}) copy-start(bf16[128,2048]{1,0:T(8,128)(2,1)} %param.7) | copy-start | bytes 1572868
  7.2 2.2 copy-start.7
  7.2 162.6 %all-gather.2.cloned.1.call-start = ((), (), s32[]{:S(2)}) async-start(), calls=%async_computation.5 | async-start | bytes 7077888 | tf_op jit(solution)/shard_map/all_gather | solution.py:75
  14.3 15.3 %copy-start.8 = (f32[128,2]{0,1:T(2,128)S(1)}, f32[128,2]{0,1:T(2,128)}, u32[]{:S(2)}) copy-start(f32[128,2]{0,1:T(2,128)} %param.9) | copy-start | bytes 3076
  14.3 15.8 %copy-start.4 = (bf16[128,2048]{1,0:T(8,128)(2,1)S(1)}, bf16[128,2048]{1,0:T(8,128)(2,1)}, u32[]{:S(2)}) copy-start(bf16[128,2048]{1,0:T(8,128)(2,1)} %param.8) | copy-start | bytes 1572868
  14.3 78.2 %all-to-all-start.1 = ((bf16[2,2,80,2048]{3,1,0,2:T(2,128)(2,1)}), bf16[2,2,80,2048]{3,1,0,2:T(2,128)(2,1)S(1)}, u32[]{:S(2)}, u32[]{:S(2)}) async-start(bf16[2,2,80,2048]{3,1,0,2:T(2,128)(2,1)} %copy.106), calls=%async_computation.1 | async-start | bytes 2621440 | tf_op jit(solution)/shard_map/all_to_all | solution.py:24
  30.7 4.0 %collective-permute-start = (bf16[1,2,80,2048]{3,2,1,0:T(8,128)(2,1)S(1)}, bf16[1,2,80,2048]{3,2,1,0:T(8,128)(2,1)S(1)}, u32[]{:S(2)}, u32[]{:S(2)}) collective-permute-start(bf16[1,2,80,2048]{3,2,1,0:T(8,128)(2,1)S(1)} %bitcast.106), channel_id=1, source_target_pairs={{0,1},{1,0},{2,3},{3,2},{4,5},{5,4},{6,7},{7,6},{8,9},{9,8},{10,11... | collective-permute-start | bytes 1966088 | tf_op jit(solution)/shard_map/ppermute | solution.py:18
  34.8 24.2 %collective-permute-start.1 = (bf16[2,1,80,2048]{3,2,1,0:T(8,128)(2,1)S(1)}, bf16[2,1,80,2048]{3,2,1,0:T(8,128)(2,1)S(1)}, u32[]{:S(2)}, u32[]{:S(2)}) collective-permute-start(bf16[2,1,80,2048]{3,2,1,0:T(8,128)(2,1)S(1)} %get-tuple-element.9), channel_id=1, source_target_pairs={{0,32},{32,0},{1,33},{33,1},{2,34},{34,2},{3,35},{35,3},{4,36},{36... | collective-permute-start | bytes 1966088 | tf_op jit(solution)/shard_map/ppermute | solution.py:18
  92.5 67.2 %all-to-all-start = ((bf16[2,2,80,2048]{3,1,0,2:T(2,128)(2,1)}), bf16[2,2,80,2048]{3,1,0,2:T(2,128)(2,1)S(1)}, u32[]{:S(2)}, u32[]{:S(2)}) async-start(bf16[2,2,80,2048]{3,1,0,2:T(2,128)(2,1)} %copy.104), calls=%async_computation | async-start | bytes 2621440 | tf_op jit(solution)/shard_map/all_to_all | solution.py:28
  98.7 21.0 %collective-permute-start.2 = (bf16[1,256,768]{2,1,0:T(8,128)(2,1)}, bf16[1,256,768]{2,1,0:T(8,128)(2,1)}, u32[]{:S(2)}, u32[]{:S(2)}) collective-permute-start(bf16[1,256,768]{2,1,0:T(8,128)(2,1)} %param.13), channel_id=1, source_target_pairs={{0,64},{64,0},{1,65},{65,1},{2,66},{66,2},{3,67},{67,3},{4,68},{68... | collective-permute-start | bytes 1179656 | tf_op jit(solution)/shard_map/ppermute | solution.py:49
  103.8 21.7 %collective-permute-start.4 = (bf16[1,256,768]{2,1,0:T(8,128)(2,1)}, bf16[1,256,768]{2,1,0:T(8,128)(2,1)}, u32[]{:S(2)}, u32[]{:S(2)}) collective-permute-start(bf16[1,256,768]{2,1,0:T(8,128)(2,1)} %param.13), channel_id=1, source_target_pairs={{0,384},{128,0},{256,128},{384,256},{1,385},{129,1},{257,129},{385... | collective-permute-start | bytes 1179656 | tf_op jit(solution)/shard_map/ppermute | solution.py:51
  106.6 23.6 %collective-permute-start.3 = (bf16[1,256,768]{2,1,0:T(8,128)(2,1)}, bf16[1,256,768]{2,1,0:T(8,128)(2,1)}, u32[]{:S(2)}, u32[]{:S(2)}) collective-permute-start(bf16[1,256,768]{2,1,0:T(8,128)(2,1)} %param.13), channel_id=1, source_target_pairs={{0,128},{128,256},{256,384},{384,0},{1,129},{129,257},{257,385},{3... | collective-permute-start | bytes 1179656 | tf_op jit(solution)/shard_map/ppermute | solution.py:50
  111.0 1.9 copy-start.5
  119.7 18.3 %collective-permute-start.5 = (bf16[1,256,768]{2,1,0:T(8,128)(2,1)}, bf16[1,256,768]{2,1,0:T(8,128)(2,1)S(1)}, u32[]{:S(2)}, u32[]{:S(2)}) collective-permute-start(bf16[1,256,768]{2,1,0:T(8,128)(2,1)} %collective-permute-done.2), channel_id=1, source_target_pairs={{0,128},{128,256},{256,384},{384,0},{1,129},{129,257},{257,385},{3... | collective-permute-start | bytes 1179656 | tf_op jit(solution)/shard_map/ppermute | solution.py:52
  122.2 29.3 %collective-permute-start.6 = (bf16[1,256,768]{2,1,0:T(8,128)(2,1)}, bf16[1,256,768]{2,1,0:T(8,128)(2,1)S(1)}, u32[]{:S(2)}, u32[]{:S(2)}) collective-permute-start(bf16[1,256,768]{2,1,0:T(8,128)(2,1)} %collective-permute-done.2), channel_id=1, source_target_pairs={{0,384},{128,0},{256,128},{384,256},{1,385},{129,1},{257,129},{385... | collective-permute-start | bytes 1179656 | tf_op jit(solution)/shard_map/ppermute | solution.py:53
  125.6 26.7 %collective-permute-start.7 = (bf16[1,256,768]{2,1,0:T(8,128)(2,1)}, bf16[1,256,768]{2,1,0:T(8,128)(2,1)S(1)}, u32[]{:S(2)}, u32[]{:S(2)}) collective-permute-start(bf16[1,256,768]{2,1,0:T(8,128)(2,1)} %collective-permute-done.4), channel_id=1, source_target_pairs={{0,384},{128,0},{256,128},{384,256},{1,385},{129,1},{257,129},{385... | collective-permute-start | bytes 1179656 | tf_op jit(solution)/shard_map/ppermute | solution.py:54
  138.0 15.1 %collective-permute-start.8 = (bf16[1,256,768]{2,1,0:T(8,128)(2,1)S(1)}, bf16[1,256,768]{2,1,0:T(8,128)(2,1)S(1)}, u32[]{:S(2)}, u32[]{:S(2)}) collective-permute-start(bf16[1,256,768]{2,1,0:T(8,128)(2,1)S(1)} %collective-permute-done.5), channel_id=1, source_target_pairs={{0,128},{128,256},{256,384},{384,0},{1,129},{129,257},{257,385},{3... | collective-permute-start | bytes 1179656 | tf_op jit(solution)/shard_map/ppermute | solution.py:55
  144.6 4.0 %collective-permute-start.9 = (bf16[1,2,80,2048]{3,2,1,0:T(8,128)(2,1)S(1)}, bf16[1,2,80,2048]{3,2,1,0:T(8,128)(2,1)S(1)}, u32[]{:S(2)}, u32[]{:S(2)}) collective-permute-start(bf16[1,2,80,2048]{3,2,1,0:T(8,128)(2,1)S(1)} %copy.115), channel_id=1, source_target_pairs={{0,1},{1,0},{2,3},{3,2},{4,5},{5,4},{6,7},{7,6},{8,9},{9,8},{10,11... | collective-permute-start | bytes 1966088 | tf_op jit(solution)/shard_map/ppermute | solution.py:18
  148.7 18.8 %collective-permute-start.10 = (bf16[2,1,80,2048]{3,2,1,0:T(8,128)(2,1)S(1)}, bf16[2,1,80,2048]{3,2,1,0:T(8,128)(2,1)}, u32[]{:S(2)}, u32[]{:S(2)}) collective-permute-start(bf16[2,1,80,2048]{3,2,1,0:T(8,128)(2,1)S(1)} %get-tuple-element.5), channel_id=1, source_target_pairs={{0,32},{32,0},{1,33},{33,1},{2,34},{34,2},{3,35},{35,3},{4,36},{36... | collective-permute-start | bytes 1966088 | tf_op jit(solution)/shard_map/ppermute | solution.py:18
  169.8 4.1 %copy-start.2 = (bf16[2,2048,768]{2,1,0:T(8,128)(2,1)S(1)}, bf16[2,2048,768]{2,1,0:T(8,128)(2,1)}, u32[]{:S(2)}) copy-start(bf16[2,2048,768]{2,1,0:T(8,128)(2,1)} %all-gather.2.cloned.1.call-done) | copy-start | bytes 18874372
  173.9 2.9 copy-start.11
  173.9 2.9 copy-start.3
  176.8 3.7 %copy-start.12 = (f32[320,768]{1,0:T(8,128)}, f32[320,768]{1,0:T(8,128)S(1)}, u32[]{:S(2)}) copy-start(f32[320,768]{1,0:T(8,128)S(1)} %fusion.1) | copy-start | bytes 2949124
  180.5 0.8 copy-start.9
  183.5 71.7 %all-to-all-start.2 = ((bf16[2,2,80,1024]{3,1,0,2:T(2,128)(2,1)}), bf16[2,2,80,1024]{3,1,0,2:T(2,128)(2,1)S(1)}, u32[]{:S(2)}, u32[]{:S(2)}) async-start(bf16[2,2,80,1024]{3,1,0,2:T(2,128)(2,1)} %copy.109), calls=%async_computation.2 | async-start | bytes 1310720 | tf_op jit(solution)/shard_map/all_to_all | solution.py:34
  195.2 108.9 %reduce-scatter.2.cloned.1.call-start = ((), (), s32[]{:S(2)}) async-start(), calls=%async_computation.6 | async-start | bytes 1966080 | tf_op jit(solution)/shard_map/reduce_scatter | solution.py:138
  198.7 1.7 copy-start.1
  198.7 4.4 %copy-start.10 = (bf16[320,768]{1,0:T(8,128)(2,1)S(1)}, bf16[320,768]{1,0:T(8,128)(2,1)}, u32[]{:S(2)}) copy-start(bf16[320,768]{1,0:T(8,128)(2,1)} %copy-done.9) | copy-start | bytes 1474564
  200.4 48.7 %collective-permute-start.15 = (bf16[4,256,768]{2,1,0:T(8,128)(2,1)S(1)}, bf16[4,256,768]{2,1,0:T(8,128)(2,1)}, u32[]{:S(2)}, u32[]{:S(2)}) collective-permute-start(bf16[4,256,768]{2,1,0:T(8,128)(2,1)S(1)} %dynamic-slice_bitcast_fusion), channel_id=1, source_target_pairs={{0,64},{64,0},{1,65},{65,1},{2,66},{66,2},{3,67},{67,3},{4,68},{68... | collective-permute-start | bytes 4718600 | tf_op jit(solution)/shard_map/ppermute | solution.py:136
  208.2 36.3 %collective-permute-start.13 = (bf16[2,1,80,1024]{3,2,1,0:T(8,128)(2,1)}, bf16[2,1,80,1024]{3,2,1,0:T(8,128)(2,1)S(1)}, u32[]{:S(2)}, u32[]{:S(2)}) collective-permute-start(bf16[2,1,80,1024]{3,2,1,0:T(8,128)(2,1)} %get-tuple-element.19), channel_id=1, source_target_pairs={{0,32},{32,0},{1,33},{33,1},{2,34},{34,2},{3,35},{35,3},{4,36},{36... | collective-permute-start | bytes 983048 | tf_op jit(solution)/shard_map/ppermute | solution.py:18
  244.5 0.7 copy-start.6
  247.2 5.4 %collective-permute-start.14 = (bf16[1,2,80,1024]{3,2,1,0:T(8,128)(2,1)}, bf16[1,2,80,1024]{3,2,1,0:T(8,128)(2,1)}, u32[]{:S(2)}, u32[]{:S(2)}) collective-permute-start(bf16[1,2,80,1024]{3,2,1,0:T(8,128)(2,1)} %get-tuple-element.17), channel_id=1, source_target_pairs={{0,1},{1,0},{2,3},{3,2},{4,5},{5,4},{6,7},{7,6},{8,9},{9,8},{10,11... | collective-permute-start | bytes 983048 | tf_op jit(solution)/shard_map/ppermute | solution.py:18
  255.2 47.6 %all-to-all-start.3 = ((bf16[2,2,80,1024]{3,1,0,2:T(2,128)(2,1)}), bf16[2,2,80,1024]{3,1,0,2:T(2,128)(2,1)S(1)}, u32[]{:S(2)}, u32[]{:S(2)}) async-start(bf16[2,2,80,1024]{3,1,0,2:T(2,128)(2,1)} %copy.112), calls=%async_computation.3 | async-start | bytes 1310720 | tf_op jit(solution)/shard_map/all_to_all | solution.py:38
  268.0 11.7 %collective-permute-start.11 = (bf16[2,1,80,1024]{3,2,1,0:T(8,128)(2,1)S(1)}, bf16[2,1,80,1024]{3,2,1,0:T(8,128)(2,1)S(1)}, u32[]{:S(2)}, u32[]{:S(2)}) collective-permute-start(bf16[2,1,80,1024]{3,2,1,0:T(8,128)(2,1)S(1)} %copy.117), channel_id=1, source_target_pairs={{0,32},{32,0},{1,33},{33,1},{2,34},{34,2},{3,35},{35,3},{4,36},{36... | collective-permute-start | bytes 983048 | tf_op jit(solution)/shard_map/ppermute | solution.py:18
  279.8 3.5 %collective-permute-start.12 = (bf16[1,2,80,1024]{3,2,1,0:T(8,128)(2,1)S(1)}, bf16[1,2,80,1024]{3,2,1,0:T(8,128)(2,1)S(1)}, u32[]{:S(2)}, u32[]{:S(2)}) collective-permute-start(bf16[1,2,80,1024]{3,2,1,0:T(8,128)(2,1)S(1)} %get-tuple-element.13), channel_id=1, source_target_pairs={{0,1},{1,0},{2,3},{3,2},{4,5},{5,4},{6,7},{7,6},{8,9},{9,8},{10,11... | collective-permute-start | bytes 983048 | tf_op jit(solution)/shard_map/ppermute | solution.py:18
Sparse Core Ops, SparseCore 0:
  11.2 125.6 all-gather.1
  252.7 32.8 reduce-scatter.1
